TPU v7x, 32 devices: a whole 2x2x4 slice. The times are simulated.
32 devices in a mesh: parts: 2 (over x), rows: 2 (over core), cols: 8 (over z, y).
Axes of the slice: x: 2, y: 2, z: 4, core: 2. Of those that a mesh axis runs over, the one named last changes fastest.
Arguments:
- src_feat: float32 [32, 131072], P(None, ('parts', 'rows', 'cols')), parts along dimension 1, may hold values from -0.75 to 0.75
- tgt_feat: float32 [32, 16384], P(None, ('parts', 'cols')), parts along dimension 1, may hold values from -0.75 to 0.75
- tgt_pot: float32 [16384], P(('parts', 'cols')), parts along dimension 0, may hold values from -25 to 25
- log_src: float32 [131072], P(('parts', 'rows', 'cols')), parts along dimension 0, may hold values from -3 to 3
- log_tgt: float32 [16384], P(('parts', 'cols')), parts along dimension 0, may hold values from -3 to 3
- pairs: int32 [512, 24], P(('parts', 'rows', 'cols')), parts along dimension 0, may hold values from 0 to 31, as said below
- counts: int32 [512], P(('parts', 'rows', 'cols')), parts along dimension 0, may hold values from 1 to 24, as said below
Outputs:
- src_pot: float32 [131072], P(('parts', 'rows', 'cols')), parts along dimension 0
- new_tgt_pot: float32 [16384], P(('parts', 'cols')), parts along dimension 0
There are 2 independent parts, one for each index of `parts`. A program takes and returns all parts, laid end to end along the dimension named above; each array names one. Nothing has to cross between parts.
Inputs may be any that keep to these rules, and one draw needn't show every extreme that they name: `pairs`: each row names 24 different target blocks, and every target block is the first entry of some row. `counts`: row 0 uses all 24 entries and row 1 only one.
All inputs are finite; a program needn't handle non-finite values.
Results may differ from a plain program's by a relative error of at most 0.0003.
Values sent between devices are 32-bit elements; how exact they have to be, the bound alone decides.
No kernel may reach another device: no remote copies, remote signals or barrier semaphores. Data moves between devices by JAX's collectives and lax.ppermute only.
A program may use at most 128 MiB of HBM per device.

v0:
```python
import functools

import jax
import jax.numpy as jnp
from jax import lax
from jax.experimental import pallas as pl
from jax.experimental.pallas import tpu as pltpu
from jax.sharding import PartitionSpec as P

BLK = 256
KP = 128
LANE = 128

epsilon = 0.1
NEG = -1e30
LOG2E = 1.4426950408889634
LN2 = 0.6931471805599453


def split3(v):
    first = lax.reduce_precision(v, exponent_bits=8, mantissa_bits=7)
    rest = v - first
    second = lax.reduce_precision(rest, exponent_bits=8, mantissa_bits=7)
    third = rest - second
    return (first.astype(jnp.bfloat16), second.astype(jnp.bfloat16),
            third.astype(jnp.bfloat16))


def split3_kernel(v):
    first = v.astype(jnp.bfloat16)
    rest = v - first.astype(jnp.float32)
    second = rest.astype(jnp.bfloat16)
    third = (rest - second.astype(jnp.float32)).astype(jnp.bfloat16)
    return first, second, third


def build_table(d, blocks_ref, tab_ref):
    scale = 2.0 * LOG2E / epsilon
    slot_row = lax.broadcasted_iota(jnp.int32, (16, BLK), 0)
    used = 3 * d + 16

    def one(tb, carry):
        blk = blocks_ref[tb]
        y = blk[0:d, :]
        yn = jnp.sum(y * y, axis=0, keepdims=True)
        tp = blk[d:d + 1, :]
        lt = blk[d + 1:d + 2, :]
        acol = (lt + (tp - yn) / epsilon) * LOG2E
        ccol = (-yn / epsilon) * LOG2E
        y1, y2, y3 = split3_kernel(y * scale)
        for k, piece in enumerate([y1, y2, y1]):
            tab_ref[tb, k * d:(k + 1) * d, :] = piece
        slot = jnp.zeros((16, BLK), jnp.float32)
        pieces = list(split3_kernel(acol)) + list(split3_kernel(ccol))
        for k, piece in enumerate(pieces):
            slot = jnp.where(slot_row == k, piece.astype(jnp.float32), slot)
        slot = jnp.where((slot_row >= 6) & (slot_row < 9), 1.0, slot)
        tab_ref[tb, 3 * d:used, :] = slot.astype(jnp.bfloat16)
        tab_ref[tb, used:KP, :] = jnp.zeros((KP - used, BLK), jnp.bfloat16)
        return carry

    lax.fori_loop(0, tab_ref.shape[0], one, 0)


def sinkhorn_kernel(npairs, d, pairs_ref, counts_ref, xt_ref, expand_ref, sel_ref,
                    blocks_ref, fpot_ref, gtop_ref, gsum_ref, sbuf, xr_ref, xc_ref, acc_ref, tab_ref):
    b = pl.program_id(0)

    @pl.when(b == 0)
    def _init():
        gtop_ref[...] = jnp.full(gtop_ref.shape, NEG, jnp.float32)
        gsum_ref[...] = jnp.zeros(gsum_ref.shape, jnp.float32)
        build_table(d, blocks_ref, tab_ref)

    cnt = counts_ref[b]
    base = b * npairs
    xfull = xt_ref[...]
    xs = xfull[:, :d]
    ls = xfull[:, d:d + 1]
    xn = jnp.sum(xs * xs, axis=1, keepdims=True)
    x1, x2, x3 = split3_kernel(xs)
    xa = (jnp.dot(x1, expand_ref[0], preferred_element_type=jnp.float32)
          + jnp.dot(x2, expand_ref[1], preferred_element_type=jnp.float32)
          + jnp.dot(x3, expand_ref[2], preferred_element_type=jnp.float32))
    sel = sel_ref[...]
    xr_ref[...] = (xa + sel[0:1, :]).astype(jnp.bfloat16)
    acc_ref[0] = jnp.full((BLK, LANE), NEG, jnp.float32)
    acc_ref[1] = jnp.zeros((BLK, LANE), jnp.float32)

    def pairs_of(body):
        def two(k, carry):
            body([2 * k, 2 * k + 1])
            return carry

        lax.fori_loop(0, cnt // 2, two, 0)

        @pl.when(cnt % 2 == 1)
        def _last():
            body([cnt - 1])

    def quads_of(body):
        def four(k, carry):
            body([4 * k + i for i in range(4)])
            return carry

        lax.fori_loop(0, cnt // 4, four, 0)
        done = cnt - cnt % 4

        @pl.when(cnt % 4 >= 2)
        def _pair():
            body([done, done + 1])

        @pl.when(cnt % 2 == 1)
        def _last():
            body([cnt - 1])

    def row_pass(ts):
        halves = []
        for t in ts:
            s = jnp.dot(xr_ref[...], tab_ref[pairs_ref[base + t]], preferred_element_type=jnp.float32)
            halves += [s[:, :LANE], s[:, LANE:]]
        old = acc_ref[0]
        new = old
        for h in halves:
            new = jnp.maximum(new, h)
        total = acc_ref[1] * jnp.exp2(old - new)
        for h in halves:
            total = total + jnp.exp2(h - new)
        acc_ref[0] = new
        acc_ref[1] = total

    pairs_of(row_pass)
    lane_top = acc_ref[0]
    m = jnp.max(lane_top, axis=1, keepdims=True)
    lane_sum = acc_ref[1] * jnp.exp2(lane_top - m)
    lse = m + jnp.log2(jnp.sum(lane_sum, axis=1, keepdims=True))
    fpot_ref[...] = xn - (epsilon * LN2) * lse
    p1, p2, p3 = split3_kernel(ls * LOG2E - lse)
    xc_ref[...] = (xa + sel[1:2, :] + p1.astype(jnp.float32) * sel[2:3, :]
                   + p2.astype(jnp.float32) * sel[3:4, :]
                   + p3.astype(jnp.float32) * sel[4:5, :]).astype(jnp.bfloat16)

    def col_pass(ts):
        for slot, t in enumerate(ts):
            tb = pairs_ref[base + t]
            u = jnp.dot(xc_ref[...], tab_ref[tb], preferred_element_type=jnp.float32)
            sbuf[slot] = u
            cm = jnp.max(u, axis=0, keepdims=True)
            cs = jnp.sum(jnp.exp2(sbuf[slot] - cm), axis=0, keepdims=True)
            old = gtop_ref[tb]
            new = jnp.maximum(old, cm)
            gsum_ref[tb] = gsum_ref[tb] * jnp.exp2(old - new) + cs * jnp.exp2(cm - new)
            gtop_ref[tb] = new

    quads_of(col_pass)


def merge(tops, sums, axis):
    top = jnp.max(tops, axis=axis, keepdims=True)
    total = jnp.sum(sums * jnp.exp2(tops - top), axis=axis, keepdims=True)
    return top, total


def on_device(src_feat, tgt_feat, tgt_pot, log_src, log_tgt, pairs, counts):
    d = src_feat.shape[0]
    ns = src_feat.shape[1]
    nrb = ns // BLK
    npairs = pairs.shape[1]
    own_targets = tgt_feat.shape[1]
    ncols = lax.axis_size("cols")

    packed = jnp.concatenate([tgt_feat, tgt_pot[None, :], log_tgt[None, :]], axis=0)
    rowsp = packed.shape[0]
    nrows = lax.axis_size("rows")
    share = rowsp // nrows
    mine = lax.dynamic_slice_in_dim(packed, lax.axis_index("rows") * share, share, 0)
    halves = mine[None]
    col_index = lax.axis_index("cols")
    step = 1
    while step < ncols:
        partner = lax.ppermute(halves, "cols", [(i, i ^ step) for i in range(ncols)])
        low = (col_index & step) == 0
        halves = jnp.concatenate(
            [jnp.where(low, halves, partner), jnp.where(low, partner, halves)], axis=0)
        step *= 2
    other = lax.ppermute(halves, "rows", [(0, 1), (1, 0)])
    first = lax.axis_index("rows") == 0
    gathered = jnp.concatenate(
        [jnp.where(first, halves, other), jnp.where(first, other, halves)], axis=1)
    nt = ncols * own_targets
    tblocks = nt // BLK
    blocks = jnp.transpose(
        gathered.reshape(ncols, rowsp, own_targets // BLK, BLK), (0, 2, 1, 3)).reshape(tblocks, rowsp, BLK)

    col = jnp.arange(KP, dtype=jnp.int32)[None, :]
    comp = jnp.arange(d, dtype=jnp.int32)[:, None]
    def place(starts):
        hit = jnp.zeros((d, KP), bool)
        for s in starts:
            hit = hit | (col == comp + s)
        return hit.astype(jnp.bfloat16)
    expand = jnp.stack([place([0, d]), place([2 * d]), place([])])
    k0 = 3 * d
    sel = jnp.stack([
        ((col[0] >= k0) & (col[0] < k0 + 3)),
        ((col[0] >= k0 + 3) & (col[0] < k0 + 6)),
        col[0] == k0 + 6, col[0] == k0 + 7, col[0] == k0 + 8,
        col[0] < 0, col[0] < 0, col[0] < 0,
    ]).astype(jnp.float32)

    kept = (nrb // 2) * BLK
    kept_blocks = nrb // 2
    swap = [(0, 1), (1, 0)]
    feats = jnp.concatenate([src_feat, log_src[None, :]], axis=0)
    feats = jnp.concatenate([feats[:, :kept], lax.ppermute(feats[:, kept:], "rows", swap)], axis=1)
    lists = jnp.concatenate([pairs, counts[:, None]], axis=1)
    lists = jnp.concatenate([lists[:kept_blocks], lax.ppermute(lists[kept_blocks:], "rows", swap)], axis=0)
    src_feat = feats[:d]
    pairs = lists[:, :npairs]
    counts = lists[:, npairs]
    xt = jnp.transpose(feats)

    grid_spec = pltpu.PrefetchScalarGridSpec(
        num_scalar_prefetch=2,
        grid=(nrb,),
        in_specs=[
            pl.BlockSpec((BLK, d + 1), lambda b, pr, ct: (b, 0)),
            pl.BlockSpec((3, d, KP), lambda b, pr, ct: (0, 0, 0)),
            pl.BlockSpec((8, KP), lambda b, pr, ct: (0, 0)),
            pl.BlockSpec((tblocks, rowsp, BLK), lambda b, pr, ct: (0, 0, 0)),
        ],
        out_specs=[
            pl.BlockSpec((BLK, 1), lambda b, pr, ct: (b, 0)),
            pl.BlockSpec((tblocks, 1, BLK), lambda b, pr, ct: (0, 0, 0)),
            pl.BlockSpec((tblocks, 1, BLK), lambda b, pr, ct: (0, 0, 0)),
        ],
        scratch_shapes=[pltpu.VMEM((4, BLK, BLK), jnp.float32),
                        pltpu.VMEM((BLK, KP), jnp.bfloat16),
                        pltpu.VMEM((BLK, KP), jnp.bfloat16),
                        pltpu.VMEM((2, BLK, LANE), jnp.float32),
                        pltpu.VMEM((tblocks, KP, BLK), jnp.bfloat16)],
    )
    fpot, gtop, gsum = pl.pallas_call(
        functools.partial(sinkhorn_kernel, npairs, d),
        grid_spec=grid_spec,
        out_shape=[
            jax.ShapeDtypeStruct((ns, 1), jnp.float32),
            jax.ShapeDtypeStruct((tblocks, 1, BLK), jnp.float32),
            jax.ShapeDtypeStruct((tblocks, 1, BLK), jnp.float32),
        ],
        compiler_params=pltpu.CompilerParams(
            dimension_semantics=("arbitrary",), vmem_limit_bytes=100 * 1024 * 1024),
    )(pairs.reshape(-1), counts, xt, expand, sel, blocks)

    done = fpot.reshape(-1)
    src_pot = jnp.concatenate([done[:kept], lax.ppermute(done[kept:], "rows", swap)])
    parts = jnp.stack([gtop.reshape(ncols, own_targets), gsum.reshape(ncols, own_targets)], axis=1)
    mine = lax.all_to_all(parts, "cols", 0, 0, tiled=True)
    top, total = merge(mine[:, 0, :], mine[:, 1, :], 0)
    here = jnp.concatenate([top, total], axis=0)
    there = lax.ppermute(here, "rows", [(0, 1), (1, 0)])
    both = jnp.stack([jnp.where(first, here, there), jnp.where(first, there, here)])
    top, total = merge(both[:, 0, :], both[:, 1, :], 0)
    new_tgt_pot = (-epsilon * LN2) * (top[0] + jnp.log2(total[0]))
    return (src_pot, new_tgt_pot)


def solution(mesh):
    placed = (
        P(None, ("parts", "rows", "cols")),
        P(None, ("parts", "cols")),
        P(("parts", "cols")),
        P(("parts", "rows", "cols")),
        P(("parts", "cols")),
        P(("parts", "rows", "cols"), None),
        P(("parts", "rows", "cols")),
    )
    return jax.shard_map(
        on_device,
        mesh=mesh,
        in_specs=placed,
        out_specs=(P(("parts", "rows", "cols")), P(("parts", "cols"))),
        check_vma=False,
    )
```

profile of v0, /device:TPU:0, one launch (start us, length us, event | category | flops | bytes accessed | tf_op | source)
XLA Modules:
  0.0 146.0 jit_solution(187904846244961092)
XLA Ops:
  0.6 0.7 copy.23
  1.4 0.8 fusion.22
  2.1 0.5 collective-permute-start
  2.6 1.0 fusion.6
  3.6 2.6 %collective-permute-start.2 = (f32[1,17,1024]{2,0,1:T(1,128)S(1)}, f32[1,17,1024]{2,0,1:T(1,128)S(1)}, u32[]{:S(2)}, u32[]{:S(2)}) collective-permute-start(f32[1,17,1024]{2,0,1:T(1,128)S(1)} %broadcast_in_dim.28), channel_id=1, source_target_pairs={{0,1},{1,0},{2,3},{3,2},{4,5},{5,4},{6,7},{7,6},{8,9},{9,8},{10,11... | collective-permute-start | bytes 208904 | tf_op jit(solution)/shard_map/ppermute | solution.py:181
  6.2 1.1 fusion.1
  7.3 0.2 collective-permute-start.1
  7.5 0.1 fusion.13
  7.6 1.4 collective-permute-done.2
  9.0 0.1 broadcast_select_fusion.3
  9.1 0.1 pad_maximum_fusion.5
  9.2 1.9 %collective-permute-start.3 = (f32[2,17,1024]{2,0,1:T(2,128)S(1)}, f32[2,17,1024]{2,0,1:T(2,128)S(1)}, u32[]{:S(2)}, u32[]{:S(2)}) collective-permute-start(f32[2,17,1024]{2,0,1:T(2,128)S(1)} %pad_maximum_fusion.5), channel_id=1, source_target_pairs={{0,2},{1,3},{2,0},{3,1},{4,6},{5,7},{6,4},{7,5},{8,10},{9,11},{10,... | collective-permute-start | bytes 417800 | tf_op jit(solution)/shard_map/ppermute | solution.py:181
  11.1 3.6 %collective-permute-done.3 = f32[2,17,1024]{2,0,1:T(2,128)S(1)} collective-permute-done((f32[2,17,1024]{2,0,1:T(2,128)S(1)}, f32[2,17,1024]{2,0,1:T(2,128)S(1)}, u32[]{:S(2)}, u32[]{:S(2)}) %collective-permute-start.3) | collective-permute-done | bytes 139296 | tf_op jit(solution)/shard_map/ppermute | solution.py:181
  14.7 0.2 broadcast_select_fusion.5
  14.9 0.1 pad_maximum_fusion.4
  15.0 2.7 %collective-permute-start.4 = (f32[4,17,1024]{2,0,1:T(4,128)S(1)}, f32[4,17,1024]{2,0,1:T(4,128)S(1)}, u32[]{:S(2)}, u32[]{:S(2)}) collective-permute-start(f32[4,17,1024]{2,0,1:T(4,128)S(1)} %pad_maximum_fusion.4), channel_id=1, source_target_pairs={{0,4},{1,5},{2,6},{3,7},{4,0},{5,1},{6,2},{7,3},{8,12},{9,13},{10,... | collective-permute-start | bytes 835592 | tf_op jit(solution)/shard_map/ppermute | solution.py:181
  17.8 0.6 convert_element_type.25.sel_ref
  18.4 0.1 pad.25.clone
  18.5 0.7 maximum_maximum_fusion.expand_ref
  19.1 10.4 %collective-permute-done.4 = f32[4,17,1024]{2,0,1:T(4,128)S(1)} collective-permute-done((f32[4,17,1024]{2,0,1:T(4,128)S(1)}, f32[4,17,1024]{2,0,1:T(4,128)S(1)}, u32[]{:S(2)}, u32[]{:S(2)}) %collective-permute-start.4) | collective-permute-done | bytes 278560 | tf_op jit(solution)/shard_map/ppermute | solution.py:181
  29.5 0.2 broadcast_select_fusion.7
  29.7 0.1 pad_maximum_fusion.2
  29.8 0.1 collective-permute-start.5
  29.9 0.0 collective-permute-done
  29.9 0.7 reshape.162.pairs_ref
  30.6 0.7 fusion.19.counts_ref
  31.3 0.0 collective-permute-done.1
  31.4 2.0 %copy.24 = f32[33,4096]{0,1:T(8,128)} copy(f32[33,4096]{1,0:T(8,128)S(1)} %pad_maximum_fusion.1) | data formatting | bytes 1081344 | tf_op jit(solution)/shard_map/concatenate | solution.py:215
  33.3 0.0 collective-permute-done.5
  33.3 0.2 broadcast_select_fusion.1
  33.5 0.1 fusion.3
  33.6 0.1 fusion
  33.7 0.4 copy.25
  34.0 1.2 reshape.163.blocks_ref
  35.2 83.2 %shard_map.86 = (f32[4096,1]{1,0:T(8,128)}, f32[32,1,256]{2,1,0:T(1,128)}, f32[32,1,256]{2,1,0:T(1,128)}) custom-call(s32[384]{0:T(512)} %reshape.162.pairs_ref, s32[16]{0:T(128)} %fusion.19.counts_ref, f32[4096,33]{1,0:T(8,128)} %bitcast.40, bf16[3,32,128]{2,1,0:T(8,128)(2,1)} %maximum_maximum_fusion.expand_ref, f32[8,128]{1,0:T(8,128)} %convert_element_type.25.sel_ref, ...), custom_call_target="tpu_custom_call" | custom-call | tf_op jit(solution)/shard_map/pallas_call | solution.py:243
  118.4 1.5 %pad_maximum_fusion.6 = f32[8,2,1024]{2,1,0:T(2,128)} fusion(f32[8,1,1024]{2,1,0:T(1,128)} %bitcast.46, f32[8,1,1024]{2,1,0:T(1,128)} %bitcast.45), kind=kLoop, calls=%fused_computation.34 | loop fusion | flops 16384 | bytes 131072 | tf_op jit(solution)/shard_map/stack | solution.py:257
  119.9 17.1 %all-to-all-start = ((f32[8,2,1024]{2,1,0:T(2,128)}), f32[8,2,1024]{2,1,0:T(2,128)S(1)}, u32[]{:S(2)}, u32[]{:S(2)}) async-start(f32[8,2,1024]{2,1,0:T(2,128)} %pad_maximum_fusion.6), calls=%async_computation | async-start | bytes 131072 | tf_op jit(solution)/shard_map/all_to_all | solution.py:258
  137.0 2.1 %slice_reduce_fusion.1 = (f32[2048]{0:T(1024)S(1)}, f32[2048]{0:T(1024)S(1)}) fusion(f32[4096,1]{1,0:T(8,128)} %get-tuple-element.5), kind=kLoop, calls=%fused_computation.9 | loop fusion | bytes 32768 | tf_op jit(solution)/shard_map/slice | solution.py:256
  139.2 0.1 collective-permute-start.6
  139.2 4.7 %all-to-all-done = f32[8,2,1024]{2,1,0:T(2,128)S(1)} async-done(((f32[8,2,1024]{2,1,0:T(2,128)}), f32[8,2,1024]{2,1,0:T(2,128)S(1)}, u32[]{:S(2)}, u32[]{:S(2)}) %all-to-all-start) | async-done | bytes 65568 | tf_op jit(solution)/shard_map/all_to_all | solution.py:258
  143.9 0.1 slice_reduce_fusion.2
  144.0 0.1 collective-permute-start.7
  144.1 0.0 collective-permute-done.6
  144.1 0.6 pad_maximum_fusion.7
  144.7 0.5 collective-permute-done.7
  145.4 0.6 add_multiply_fusion
  (17 shorter events, 0.3 us)
Async XLA Ops:
  2.1 27.8 %collective-permute-start = (s32[8,25]{1,0:T(8,128)S(1)}, s32[8,25]{1,0:T(8,128)S(1)}, u32[]{:S(2)}, u32[]{:S(2)}) collective-permute-start(s32[8,25]{1,0:T(8,128)S(1)} %get-tuple-element.31), channel_id=1, source_target_pairs={{0,8},{8,0},{1,9},{9,1},{2,10},{10,2},{3,11},{11,3},{4,12},{12,4},... | collective-permute-start | bytes 2408 | tf_op jit(solution)/shard_map/ppermute | solution.py:217
  3.6 5.4 %collective-permute-start.2 = (f32[1,17,1024]{2,0,1:T(1,128)S(1)}, f32[1,17,1024]{2,0,1:T(1,128)S(1)}, u32[]{:S(2)}, u32[]{:S(2)}) collective-permute-start(f32[1,17,1024]{2,0,1:T(1,128)S(1)} %broadcast_in_dim.28), channel_id=1, source_target_pairs={{0,1},{1,0},{2,3},{3,2},{4,5},{5,4},{6,7},{7,6},{8,9},{9,8},{10,11... | collective-permute-start | bytes 208904 | tf_op jit(solution)/shard_map/ppermute | solution.py:181
  7.3 24.0 %collective-permute-start.1 = (f32[33,2048]{1,0:T(8,128)S(1)}, f32[33,2048]{1,0:T(8,128)S(1)}, u32[]{:S(2)}, u32[]{:S(2)}) collective-permute-start(f32[33,2048]{1,0:T(8,128)S(1)} %get-tuple-element.20), channel_id=1, source_target_pairs={{0,8},{8,0},{1,9},{9,1},{2,10},{10,2},{3,11},{11,3},{4,12},{12,4},... | collective-permute-start | bytes 811016 | tf_op jit(solution)/shard_map/ppermute | solution.py:215
  9.2 5.5 %collective-permute-start.3 = (f32[2,17,1024]{2,0,1:T(2,128)S(1)}, f32[2,17,1024]{2,0,1:T(2,128)S(1)}, u32[]{:S(2)}, u32[]{:S(2)}) collective-permute-start(f32[2,17,1024]{2,0,1:T(2,128)S(1)} %pad_maximum_fusion.5), channel_id=1, source_target_pairs={{0,2},{1,3},{2,0},{3,1},{4,6},{5,7},{6,4},{7,5},{8,10},{9,11},{10,... | collective-permute-start | bytes 417800 | tf_op jit(solution)/shard_map/ppermute | solution.py:181
  15.0 14.5 %collective-permute-start.4 = (f32[4,17,1024]{2,0,1:T(4,128)S(1)}, f32[4,17,1024]{2,0,1:T(4,128)S(1)}, u32[]{:S(2)}, u32[]{:S(2)}) collective-permute-start(f32[4,17,1024]{2,0,1:T(4,128)S(1)} %pad_maximum_fusion.4), channel_id=1, source_target_pairs={{0,4},{1,5},{2,6},{3,7},{4,0},{5,1},{6,2},{7,3},{8,12},{9,13},{10,... | collective-permute-start | bytes 835592 | tf_op jit(solution)/shard_map/ppermute | solution.py:181
  29.8 3.5 %collective-permute-start.5 = (f32[8,17,1024]{2,0,1:T(8,128)S(1)}, f32[8,17,1024]{2,0,1:T(8,128)S(1)}, u32[]{:S(2)}, u32[]{:S(2)}) collective-permute-start(f32[8,17,1024]{2,0,1:T(8,128)S(1)} %pad_maximum_fusion.2), channel_id=1, source_target_pairs={{0,8},{8,0},{1,9},{9,1},{2,10},{10,2},{3,11},{11,3},{4,12},{12,4},... | collective-permute-start | bytes 1671176 | tf_op jit(solution)/shard_map/ppermute | solution.py:186
  119.9 24.0 %all-to-all-start = ((f32[8,2,1024]{2,1,0:T(2,128)}), f32[8,2,1024]{2,1,0:T(2,128)S(1)}, u32[]{:S(2)}, u32[]{:S(2)}) async-start(f32[8,2,1024]{2,1,0:T(2,128)} %pad_maximum_fusion.6), calls=%async_computation | async-start | bytes 131072 | tf_op jit(solution)/shard_map/all_to_all | solution.py:258
  139.2 5.0 %collective-permute-start.6 = (f32[2048]{0:T(1024)S(1)}, f32[2048]{0:T(1024)S(1)}, u32[]{:S(2)}, u32[]{:S(2)}) collective-permute-start(f32[2048]{0:T(1024)S(1)} %get-tuple-element.9), channel_id=1, source_target_pairs={{0,8},{8,0},{1,9},{9,1},{2,10},{10,2},{3,11},{11,3},{4,12},{12,4},... | collective-permute-start | bytes 24584 | tf_op jit(solution)/shard_map/ppermute | solution.py:256
  144.0 1.2 collective-permute-start.7
where the time goes:
time: 147 us; the launch traced here: 146 us
  Pallas kernels  83.2 us (57%)
  starting transfers between devices  25.2 us (17%)
  waiting for transfers between devices  20.5 us (14%)
  other arithmetic  9.01 us (6%)
  local copies, waits for them, and re-layouts  7.25 us (5%)
    pallas_call x1, Pallas kernels, on_device(): pl.pallas_call(functools.partial(sinkhorn_kernel, npairs, d), grid_spec=g...  83.2 us
    all_to_all x1, starting transfers between devices, on_device(): mine = lax.all_to_all(parts, 'cols', 0, 0, tiled=True)  17.1 us
    ppermute x3, waiting for transfers between devices, on_device(): lax.ppermute(halves, 'cols', [(i, i ^ step) for i in range(ncols)])  15.3 us
    ppermute x3, starting transfers between devices, on_device(): lax.ppermute(halves, 'cols', [(i, i ^ step) for i in range(ncols)])  7.17 us
    all_to_all x1, waiting for transfers between devices, on_device(): mine = lax.all_to_all(parts, 'cols', 0, 0, tiled=True)  4.67 us
  transfers between devices with their start and end apart: 9, of which 5 were waited for; matrix products, arithmetic and copies ran while one was open for 7% of the time, Pallas kernels for 0%

commit v1 on v0

--- a/solution.py
+++ b/solution.py
@@ -176,13 +176,16 @@
     mine = lax.dynamic_slice_in_dim(packed, lax.axis_index("rows") * share, share, 0)
     halves = mine[None]
     col_index = lax.axis_index("cols")
-    step = 1
-    while step < ncols:
+    nbits = ncols.bit_length() - 1
+    for bit in reversed(range(nbits)):
+        step = 1 << bit
         partner = lax.ppermute(halves, "cols", [(i, i ^ step) for i in range(ncols)])
         low = (col_index & step) == 0
         halves = jnp.concatenate(
             [jnp.where(low, halves, partner), jnp.where(low, partner, halves)], axis=0)
-        step *= 2
+    halves = jnp.transpose(
+        halves.reshape((2,) * nbits + (share, own_targets)),
+        tuple(reversed(range(nbits))) + (nbits, nbits + 1)).reshape(ncols, share, own_targets)
     other = lax.ppermute(halves, "rows", [(0, 1), (1, 0)])
     first = lax.axis_index("rows") == 0
     gathered = jnp.concatenate(

time: 147 us -> 144 us (0.980)
  waiting for transfers between devices: 20.5 us -> 17.6 us
  Pallas kernels: 83.2 us -> 81.2 us
    ppermute x3, waiting for transfers between devices: 15.3 us -> 12.4 us  [on_device(): lax.ppermute(halves, 'cols', [(i, i ^ step) for i in range(ncols)])]
    pallas_call x1, Pallas kernels: 83.2 us -> 81.2 us  [on_device(): pl.pallas_call(functools.partial(sinkhorn_kernel, npairs, d), grid_spec=g...]
    all_to_all x1, starting transfers between devices: 17.1 us -> 18.8 us  [on_device(): mine = lax.all_to_all(parts, 'cols', 0, 0, tiled=True)]
  transfers between devices with their start and end apart: 9 -> 9, of which waited for: 5 -> 5; matrix products, arithmetic and copies ran while one was open for 7% -> 8% of each run, Pallas kernels for 0% -> 0%
where the time goes in v1:
time: 144 us; the launch traced here: 143 us
  Pallas kernels  81.2 us (56%)
  starting transfers between devices  25.5 us (18%)
  waiting for transfers between devices  17.6 us (12%)
  other arithmetic  8.97 us (6%)
  local copies, waits for them, and re-layouts  8.39 us (6%)
    pallas_call x1, Pallas kernels, on_device(): pl.pallas_call(functools.partial(sinkhorn_kernel, npairs, d), grid_spec=g...  81.2 us
    all_to_all x1, starting transfers between devices, on_device(): mine = lax.all_to_all(parts, 'cols', 0, 0, tiled=True)  18.8 us
    ppermute x3, waiting for transfers between devices, on_device(): lax.ppermute(halves, 'cols', [(i, i ^ step) for i in range(ncols)])  12.4 us
    ppermute x3, starting transfers between devices, on_device(): lax.ppermute(halves, 'cols', [(i, i ^ step) for i in range(ncols)])  5.78 us
    all_to_all x1, waiting for transfers between devices, on_device(): mine = lax.all_to_all(parts, 'cols', 0, 0, tiled=True)  4.67 us
  transfers between devices with their start and end apart: 9, of which 5 were waited for; matrix products, arithmetic and copies ran while one was open for 8% of the time, Pallas kernels for 0%

profile of v1, /device:TPU:0, one launch (start us, length us, event | category | flops | bytes accessed | tf_op | source)
XLA Modules:
  0.0 142.5 jit_solution(8535164710858575903)
XLA Ops:
  0.6 0.7 copy.30
  1.4 0.8 fusion.22
  2.1 0.5 collective-permute-start
  2.6 1.0 fusion.6
  3.6 3.7 %collective-permute-start.2 = (f32[1,17,1024]{2,0,1:T(1,128)S(1)}, f32[1,17,1024]{2,0,1:T(1,128)S(1)}, u32[]{:S(2)}, u32[]{:S(2)}) collective-permute-start(f32[1,17,1024]{2,0,1:T(1,128)S(1)} %broadcast_in_dim.28), channel_id=1, source_target_pairs={{0,4},{1,5},{2,6},{3,7},{4,0},{5,1},{6,2},{7,3},{8,12},{9,13},{10,... | collective-permute-start | bytes 208904 | tf_op jit(solution)/shard_map/ppermute | solution.py:182
  7.3 1.1 fusion.1
  8.4 0.2 collective-permute-start.1
  8.6 0.1 fusion.13
  8.7 2.9 %collective-permute-done.2 = f32[1,17,1024]{2,0,1:T(1,128)S(1)} collective-permute-done((f32[1,17,1024]{2,0,1:T(1,128)S(1)}, f32[1,17,1024]{2,0,1:T(1,128)S(1)}, u32[]{:S(2)}, u32[]{:S(2)}) %collective-permute-start.2) | collective-permute-done | bytes 69664 | tf_op jit(solution)/shard_map/ppermute | solution.py:182
  11.6 0.1 broadcast_select_fusion.3
  11.7 0.1 pad_maximum_fusion.5
  11.8 0.8 collective-permute-start.3
  12.6 4.7 %collective-permute-done.3 = f32[2,17,1024]{2,0,1:T(2,128)S(1)} collective-permute-done((f32[2,17,1024]{2,0,1:T(2,128)S(1)}, f32[2,17,1024]{2,0,1:T(2,128)S(1)}, u32[]{:S(2)}, u32[]{:S(2)}) %collective-permute-start.3) | collective-permute-done | bytes 139296 | tf_op jit(solution)/shard_map/ppermute | solution.py:182
  17.3 0.2 broadcast_select_fusion.5
  17.5 0.1 pad_maximum_fusion.4
  17.6 1.3 collective-permute-start.4
  18.9 0.6 convert_element_type.25.sel_ref
  19.5 0.1 pad.25.clone
  19.6 0.7 maximum_maximum_fusion.expand_ref
  20.3 4.9 %collective-permute-done.4 = f32[4,17,1024]{2,0,1:T(4,128)S(1)} collective-permute-done((f32[4,17,1024]{2,0,1:T(4,128)S(1)}, f32[4,17,1024]{2,0,1:T(4,128)S(1)}, u32[]{:S(2)}, u32[]{:S(2)}) %collective-permute-start.4) | collective-permute-done | bytes 278560 | tf_op jit(solution)/shard_map/ppermute | solution.py:182
  25.2 0.2 broadcast_select_fusion.7
  25.4 0.1 pad_maximum_fusion.2
  25.5 0.3 reshape.169
  25.9 0.4 copy.32
  26.3 0.4 reshape.170
  26.7 0.1 collective-permute-start.5
  26.8 0.0 collective-permute-done
  26.8 0.7 reshape.168.pairs_ref
  27.5 0.7 fusion.19.counts_ref
  28.2 0.0 collective-permute-done.1
  28.2 2.0 %copy.31 = f32[33,4096]{0,1:T(8,128)} copy(f32[33,4096]{1,0:T(8,128)S(1)} %pad_maximum_fusion.1) | data formatting | bytes 1081344 | tf_op jit(solution)/shard_map/concatenate | solution.py:218
  30.2 0.0 collective-permute-done.5
  30.2 0.1 broadcast_select_fusion.1
  30.3 0.1 fusion.3
  30.4 0.1 fusion
  30.5 0.4 copy.33
  30.9 1.2 reshape.171.blocks_ref
  32.1 81.2 %shard_map.86 = (f32[4096,1]{1,0:T(8,128)}, f32[32,1,256]{2,1,0:T(1,128)}, f32[32,1,256]{2,1,0:T(1,128)}) custom-call(s32[384]{0:T(512)} %reshape.168.pairs_ref, s32[16]{0:T(128)} %fusion.19.counts_ref, f32[4096,33]{1,0:T(8,128)} %bitcast.45, bf16[3,32,128]{2,1,0:T(8,128)(2,1)} %maximum_maximum_fusion.expand_ref, f32[8,128]{1,0:T(8,128)} %convert_element_type.25.sel_ref, ...), custom_call_target="tpu_custom_call" | custom-call | tf_op jit(solution)/shard_map/pallas_call | solution.py:246
  113.3 1.5 %pad_maximum_fusion.6 = f32[8,2,1024]{2,1,0:T(2,128)} fusion(f32[8,1,1024]{2,1,0:T(1,128)} %bitcast.52, f32[8,1,1024]{2,1,0:T(1,128)} %bitcast.51), kind=kLoop, calls=%fused_computation.34 | loop fusion | flops 16384 | bytes 131072 | tf_op jit(solution)/shard_map/stack | solution.py:260
  114.7 18.8 %all-to-all-start = ((f32[8,2,1024]{2,1,0:T(2,128)}), f32[8,2,1024]{2,1,0:T(2,128)S(1)}, u32[]{:S(2)}, u32[]{:S(2)}) async-start(f32[8,2,1024]{2,1,0:T(2,128)} %pad_maximum_fusion.6), calls=%async_computation | async-start | bytes 131072 | tf_op jit(solution)/shard_map/all_to_all | solution.py:261
  133.5 2.1 %slice_reduce_fusion.1 = (f32[2048]{0:T(1024)S(1)}, f32[2048]{0:T(1024)S(1)}) fusion(f32[4096,1]{1,0:T(8,128)} %get-tuple-element.5), kind=kLoop, calls=%fused_computation.9 | loop fusion | bytes 32768 | tf_op jit(solution)/shard_map/slice | solution.py:259
  135.7 0.1 collective-permute-start.6
  135.8 4.7 %all-to-all-done = f32[8,2,1024]{2,1,0:T(2,128)S(1)} async-done(((f32[8,2,1024]{2,1,0:T(2,128)}), f32[8,2,1024]{2,1,0:T(2,128)S(1)}, u32[]{:S(2)}, u32[]{:S(2)}) %all-to-all-start) | async-done | bytes 65568 | tf_op jit(solution)/shard_map/all_to_all | solution.py:261
  140.4 0.1 slice_reduce_fusion.2
  140.6 0.1 collective-permute-start.7
  140.6 0.0 collective-permute-done.6
  140.7 0.6 pad_maximum_fusion.7
  141.3 0.5 collective-permute-done.7
  141.9 0.6 add_multiply_fusion
  (17 shorter events, 0.3 us)
Async XLA Ops:
  2.1 24.6 %collective-permute-start = (s32[8,25]{1,0:T(8,128)S(1)}, s32[8,25]{1,0:T(8,128)S(1)}, u32[]{:S(2)}, u32[]{:S(2)}) collective-permute-start(s32[8,25]{1,0:T(8,128)S(1)} %get-tuple-element.31), channel_id=1, source_target_pairs={{0,8},{8,0},{1,9},{9,1},{2,10},{10,2},{3,11},{11,3},{4,12},{12,4},... | collective-permute-start | bytes 2408 | tf_op jit(solution)/shard_map/ppermute | solution.py:220
  3.6 7.9 %collective-permute-start.2 = (f32[1,17,1024]{2,0,1:T(1,128)S(1)}, f32[1,17,1024]{2,0,1:T(1,128)S(1)}, u32[]{:S(2)}, u32[]{:S(2)}) collective-permute-start(f32[1,17,1024]{2,0,1:T(1,128)S(1)} %broadcast_in_dim.28), channel_id=1, source_target_pairs={{0,4},{1,5},{2,6},{3,7},{4,0},{5,1},{6,2},{7,3},{8,12},{9,13},{10,... | collective-permute-start | bytes 208904 | tf_op jit(solution)/shard_map/ppermute | solution.py:182
  8.4 19.8 %collective-permute-start.1 = (f32[33,2048]{1,0:T(8,128)S(1)}, f32[33,2048]{1,0:T(8,128)S(1)}, u32[]{:S(2)}, u32[]{:S(2)}) collective-permute-start(f32[33,2048]{1,0:T(8,128)S(1)} %get-tuple-element.20), channel_id=1, source_target_pairs={{0,8},{8,0},{1,9},{9,1},{2,10},{10,2},{3,11},{11,3},{4,12},{12,4},... | collective-permute-start | bytes 811016 | tf_op jit(solution)/shard_map/ppermute | solution.py:218
  11.8 5.5 %collective-permute-start.3 = (f32[2,17,1024]{2,0,1:T(2,128)S(1)}, f32[2,17,1024]{2,0,1:T(2,128)S(1)}, u32[]{:S(2)}, u32[]{:S(2)}) collective-permute-start(f32[2,17,1024]{2,0,1:T(2,128)S(1)} %pad_maximum_fusion.5), channel_id=1, source_target_pairs={{0,2},{1,3},{2,0},{3,1},{4,6},{5,7},{6,4},{7,5},{8,10},{9,11},{10,... | collective-permute-start | bytes 417800 | tf_op jit(solution)/shard_map/ppermute | solution.py:182
  17.6 7.6 %collective-permute-start.4 = (f32[4,17,1024]{2,0,1:T(4,128)S(1)}, f32[4,17,1024]{2,0,1:T(4,128)S(1)}, u32[]{:S(2)}, u32[]{:S(2)}) collective-permute-start(f32[4,17,1024]{2,0,1:T(4,128)S(1)} %pad_maximum_fusion.4), channel_id=1, source_target_pairs={{0,1},{1,0},{2,3},{3,2},{4,5},{5,4},{6,7},{7,6},{8,9},{9,8},{10,11... | collective-permute-start | bytes 835592 | tf_op jit(solution)/shard_map/ppermute | solution.py:182
  26.7 3.5 %collective-permute-start.5 = (f32[8,17,1024]{2,0,1:T(8,128)S(1)}, f32[8,17,1024]{2,0,1:T(8,128)S(1)}, u32[]{:S(2)}, u32[]{:S(2)}) collective-permute-start(f32[8,17,1024]{2,0,1:T(8,128)S(1)} %reshape.170), channel_id=1, source_target_pairs={{0,8},{8,0},{1,9},{9,1},{2,10},{10,2},{3,11},{11,3},{4,12},{12,4},... | collective-permute-start | bytes 1671176 | tf_op jit(solution)/shard_map/ppermute | solution.py:189
  114.7 25.7 %all-to-all-start = ((f32[8,2,1024]{2,1,0:T(2,128)}), f32[8,2,1024]{2,1,0:T(2,128)S(1)}, u32[]{:S(2)}, u32[]{:S(2)}) async-start(f32[8,2,1024]{2,1,0:T(2,128)} %pad_maximum_fusion.6), calls=%async_computation | async-start | bytes 131072 | tf_op jit(solution)/shard_map/all_to_all | solution.py:261
  135.7 5.0 %collective-permute-start.6 = (f32[2048]{0:T(1024)S(1)}, f32[2048]{0:T(1024)S(1)}, u32[]{:S(2)}, u32[]{:S(2)}) collective-permute-start(f32[2048]{0:T(1024)S(1)} %get-tuple-element.9), channel_id=1, source_target_pairs={{0,8},{8,0},{1,9},{9,1},{2,10},{10,2},{3,11},{11,3},{4,12},{12,4},... | collective-permute-start | bytes 24584 | tf_op jit(solution)/shard_map/ppermute | solution.py:259
  140.6 1.2 collective-permute-start.7

commit v2 on v1

--- a/solution.py
+++ b/solution.py
@@ -84,8 +84,9 @@
           + jnp.dot(x3, expand_ref[2], preferred_element_type=jnp.float32))
     sel = sel_ref[...]
     xr_ref[...] = (xa + sel[0:1, :]).astype(jnp.bfloat16)
-    acc_ref[0] = jnp.full((BLK, LANE), NEG, jnp.float32)
-    acc_ref[1] = jnp.zeros((BLK, LANE), jnp.float32)
+    for a in range(2):
+        acc_ref[2 * a] = jnp.full((BLK, LANE), NEG, jnp.float32)
+        acc_ref[2 * a + 1] = jnp.zeros((BLK, LANE), jnp.float32)
 
     def pairs_of(body):
         def two(k, carry):
@@ -114,25 +115,32 @@
         def _last():
             body([cnt - 1])
 
-    def row_pass(ts):
+    def row_update(ts, a):
         halves = []
         for t in ts:
             s = jnp.dot(xr_ref[...], tab_ref[pairs_ref[base + t]], preferred_element_type=jnp.float32)
             halves += [s[:, :LANE], s[:, LANE:]]
-        old = acc_ref[0]
+        old = acc_ref[2 * a]
         new = old
         for h in halves:
             new = jnp.maximum(new, h)
-        total = acc_ref[1] * jnp.exp2(old - new)
+        total = acc_ref[2 * a + 1] * jnp.exp2(old - new)
         for h in halves:
             total = total + jnp.exp2(h - new)
-        acc_ref[0] = new
-        acc_ref[1] = total
-
-    pairs_of(row_pass)
-    lane_top = acc_ref[0]
+        acc_ref[2 * a] = new
+        acc_ref[2 * a + 1] = total
+
+    def row_pass(ts):
+        row_update(ts[:2], 0)
+        if len(ts) > 2:
+            row_update(ts[2:], 1)
+
+    quads_of(row_pass)
+    top_a = acc_ref[0]
+    top_b = acc_ref[2]
+    lane_top = jnp.maximum(top_a, top_b)
     m = jnp.max(lane_top, axis=1, keepdims=True)
-    lane_sum = acc_ref[1] * jnp.exp2(lane_top - m)
+    lane_sum = (acc_ref[1] * jnp.exp2(top_a - m) + acc_ref[3] * jnp.exp2(top_b - m))
     lse = m + jnp.log2(jnp.sum(lane_sum, axis=1, keepdims=True))
     fpot_ref[...] = xn - (epsilon * LN2) * lse
     p1, p2, p3 = split3_kernel(ls * LOG2E - lse)
@@ -240,7 +248,7 @@
         scratch_shapes=[pltpu.VMEM((4, BLK, BLK), jnp.float32),
                         pltpu.VMEM((BLK, KP), jnp.bfloat16),
                         pltpu.VMEM((BLK, KP), jnp.bfloat16),
-                        pltpu.VMEM((2, BLK, LANE), jnp.float32),
+                        pltpu.VMEM((4, BLK, LANE), jnp.float32),
                         pltpu.VMEM((tblocks, KP, BLK), jnp.bfloat16)],
     )
     fpot, gtop, gsum = pl.pallas_call(

time: 144 us -> 133 us (0.924); the launches traced: 143 us -> 135 us
  Pallas kernels: 81.2 us -> 77 us
  starting transfers between devices: 25.5 us -> 22.3 us
    pallas_call x1, Pallas kernels: 81.2 us -> 77 us  [on_device(): pl.pallas_call(functools.partial(sinkhorn_kernel, npairs, d), grid_spec=g...]
    all_to_all x1, starting transfers between devices: 18.8 us -> 14.9 us  [on_device(): mine = lax.all_to_all(parts, 'cols', 0, 0, tiled=True)]
  transfers between devices with their start and end apart: 9 -> 9, of which waited for: 5 -> 5; matrix products, arithmetic and copies ran while one was open for 8% -> 9% of each run, Pallas kernels for 0% -> 0%
where the time goes in v2:
time: 133 us; the launch traced here: 135 us
  Pallas kernels  77 us (58%)
  starting transfers between devices  22.3 us (17%)
  waiting for transfers between devices  17.2 us (13%)
  other arithmetic  8.97 us (7%)
  local copies, waits for them, and re-layouts  8.39 us (6%)
    pallas_call x1, Pallas kernels, on_device(): pl.pallas_call(functools.partial(sinkhorn_kernel, npairs, d), grid_spec=g...  77 us
    all_to_all x1, starting transfers between devices, on_device(): mine = lax.all_to_all(parts, 'cols', 0, 0, tiled=True)  14.9 us
    ppermute x3, waiting for transfers between devices, on_device(): lax.ppermute(halves, 'cols', [(i, i ^ step) for i in range(ncols)])  12.4 us
    ppermute x3, starting transfers between devices, on_device(): lax.ppermute(halves, 'cols', [(i, i ^ step) for i in range(ncols)])  5.78 us
    all_to_all x1, waiting for transfers between devices, on_device(): mine = lax.all_to_all(parts, 'cols', 0, 0, tiled=True)  4.24 us
  transfers between devices with their start and end apart: 9, of which 5 were waited for; matrix products, arithmetic and copies ran while one was open for 9% of the time, Pallas kernels for 0%

profile of v2, /device:TPU:0, one launch (start us, length us, event | category | flops | bytes accessed | tf_op | source)
XLA Modules:
  0.0 134.7 jit_solution(9060648758103299168)
XLA Ops:
  0.6 0.7 copy.30
  1.4 0.8 fusion.22
  2.1 0.5 collective-permute-start
  2.6 1.0 fusion.6
  3.6 3.7 %collective-permute-start.2 = (f32[1,17,1024]{2,0,1:T(1,128)S(1)}, f32[1,17,1024]{2,0,1:T(1,128)S(1)}, u32[]{:S(2)}, u32[]{:S(2)}) collective-permute-start(f32[1,17,1024]{2,0,1:T(1,128)S(1)} %broadcast_in_dim.28), channel_id=1, source_target_pairs={{0,4},{1,5},{2,6},{3,7},{4,0},{5,1},{6,2},{7,3},{8,12},{9,13},{10,... | collective-permute-start | bytes 208904 | tf_op jit(solution)/shard_map/ppermute | solution.py:190
  7.3 1.1 fusion.1
  8.4 0.2 collective-permute-start.1
  8.6 0.1 fusion.13
  8.7 2.9 %collective-permute-done.2 = f32[1,17,1024]{2,0,1:T(1,128)S(1)} collective-permute-done((f32[1,17,1024]{2,0,1:T(1,128)S(1)}, f32[1,17,1024]{2,0,1:T(1,128)S(1)}, u32[]{:S(2)}, u32[]{:S(2)}) %collective-permute-start.2) | collective-permute-done | bytes 69664 | tf_op jit(solution)/shard_map/ppermute | solution.py:190
  11.6 0.1 broadcast_select_fusion.3
  11.7 0.1 pad_maximum_fusion.5
  11.8 0.8 collective-permute-start.3
  12.6 4.7 %collective-permute-done.3 = f32[2,17,1024]{2,0,1:T(2,128)S(1)} collective-permute-done((f32[2,17,1024]{2,0,1:T(2,128)S(1)}, f32[2,17,1024]{2,0,1:T(2,128)S(1)}, u32[]{:S(2)}, u32[]{:S(2)}) %collective-permute-start.3) | collective-permute-done | bytes 139296 | tf_op jit(solution)/shard_map/ppermute | solution.py:190
  17.3 0.2 broadcast_select_fusion.5
  17.5 0.1 pad_maximum_fusion.4
  17.6 1.3 collective-permute-start.4
  18.9 0.6 convert_element_type.25.sel_ref
  19.5 0.1 pad.25.clone
  19.6 0.7 maximum_maximum_fusion.expand_ref
  20.3 4.9 %collective-permute-done.4 = f32[4,17,1024]{2,0,1:T(4,128)S(1)} collective-permute-done((f32[4,17,1024]{2,0,1:T(4,128)S(1)}, f32[4,17,1024]{2,0,1:T(4,128)S(1)}, u32[]{:S(2)}, u32[]{:S(2)}) %collective-permute-start.4) | collective-permute-done | bytes 278560 | tf_op jit(solution)/shard_map/ppermute | solution.py:190
  25.2 0.2 broadcast_select_fusion.7
  25.4 0.1 pad_maximum_fusion.2
  25.5 0.3 reshape.169
  25.9 0.4 copy.32
  26.3 0.4 reshape.170
  26.7 0.1 collective-permute-start.5
  26.8 0.0 collective-permute-done
  26.8 0.7 reshape.168.pairs_ref
  27.5 0.7 fusion.19.counts_ref
  28.2 0.0 collective-permute-done.1
  28.2 2.0 %copy.31 = f32[33,4096]{0,1:T(8,128)} copy(f32[33,4096]{1,0:T(8,128)S(1)} %pad_maximum_fusion.1) | data formatting | bytes 1081344 | tf_op jit(solution)/shard_map/concatenate | solution.py:226
  30.2 0.0 collective-permute-done.5
  30.2 0.1 broadcast_select_fusion.1
  30.3 0.1 fusion.3
  30.4 0.1 fusion
  30.5 0.4 copy.33
  30.9 1.2 reshape.171.blocks_ref
  32.1 77.0 %shard_map.86 = (f32[4096,1]{1,0:T(8,128)}, f32[32,1,256]{2,1,0:T(1,128)}, f32[32,1,256]{2,1,0:T(1,128)}) custom-call(s32[384]{0:T(512)} %reshape.168.pairs_ref, s32[16]{0:T(128)} %fusion.19.counts_ref, f32[4096,33]{1,0:T(8,128)} %bitcast.45, bf16[3,32,128]{2,1,0:T(8,128)(2,1)} %maximum_maximum_fusion.expand_ref, f32[8,128]{1,0:T(8,128)} %convert_element_type.25.sel_ref, ...), custom_call_target="tpu_custom_call" | custom-call | tf_op jit(solution)/shard_map/pallas_call | solution.py:254
  109.0 1.5 %pad_maximum_fusion.6 = f32[8,2,1024]{2,1,0:T(2,128)} fusion(f32[8,1,1024]{2,1,0:T(1,128)} %bitcast.52, f32[8,1,1024]{2,1,0:T(1,128)} %bitcast.51), kind=kLoop, calls=%fused_computation.34 | loop fusion | flops 16384 | bytes 131072 | tf_op jit(solution)/shard_map/stack | solution.py:268
  110.5 14.9 %all-to-all-start = ((f32[8,2,1024]{2,1,0:T(2,128)}), f32[8,2,1024]{2,1,0:T(2,128)S(1)}, u32[]{:S(2)}, u32[]{:S(2)}) async-start(f32[8,2,1024]{2,1,0:T(2,128)} %pad_maximum_fusion.6), calls=%async_computation | async-start | bytes 131072 | tf_op jit(solution)/shard_map/all_to_all | solution.py:269
  125.4 2.1 %slice_reduce_fusion.1 = (f32[2048]{0:T(1024)S(1)}, f32[2048]{0:T(1024)S(1)}) fusion(f32[4096,1]{1,0:T(8,128)} %get-tuple-element.5), kind=kLoop, calls=%fused_computation.9 | loop fusion | bytes 32768 | tf_op jit(solution)/shard_map/slice | solution.py:267
  127.6 0.8 collective-permute-start.6
  128.4 4.2 %all-to-all-done = f32[8,2,1024]{2,1,0:T(2,128)S(1)} async-done(((f32[8,2,1024]{2,1,0:T(2,128)}), f32[8,2,1024]{2,1,0:T(2,128)S(1)}, u32[]{:S(2)}, u32[]{:S(2)}) %all-to-all-start) | async-done | bytes 65568 | tf_op jit(solution)/shard_map/all_to_all | solution.py:269
  132.6 0.1 slice_reduce_fusion.2
  132.7 0.1 collective-permute-start.7
  132.8 0.0 collective-permute-done.6
  132.8 0.6 pad_maximum_fusion.7
  133.4 0.5 collective-permute-done.7
  134.1 0.6 add_multiply_fusion
  (17 shorter events, 0.3 us)
Async XLA Ops:
  2.1 24.6 %collective-permute-start = (s32[8,25]{1,0:T(8,128)S(1)}, s32[8,25]{1,0:T(8,128)S(1)}, u32[]{:S(2)}, u32[]{:S(2)}) collective-permute-start(s32[8,25]{1,0:T(8,128)S(1)} %get-tuple-element.31), channel_id=1, source_target_pairs={{0,8},{8,0},{1,9},{9,1},{2,10},{10,2},{3,11},{11,3},{4,12},{12,4},... | collective-permute-start | bytes 2408 | tf_op jit(solution)/shard_map/ppermute | solution.py:228
  3.6 7.9 %collective-permute-start.2 = (f32[1,17,1024]{2,0,1:T(1,128)S(1)}, f32[1,17,1024]{2,0,1:T(1,128)S(1)}, u32[]{:S(2)}, u32[]{:S(2)}) collective-permute-start(f32[1,17,1024]{2,0,1:T(1,128)S(1)} %broadcast_in_dim.28), channel_id=1, source_target_pairs={{0,4},{1,5},{2,6},{3,7},{4,0},{5,1},{6,2},{7,3},{8,12},{9,13},{10,... | collective-permute-start | bytes 208904 | tf_op jit(solution)/shard_map/ppermute | solution.py:190
  8.4 19.8 %collective-permute-start.1 = (f32[33,2048]{1,0:T(8,128)S(1)}, f32[33,2048]{1,0:T(8,128)S(1)}, u32[]{:S(2)}, u32[]{:S(2)}) collective-permute-start(f32[33,2048]{1,0:T(8,128)S(1)} %get-tuple-element.20), channel_id=1, source_target_pairs={{0,8},{8,0},{1,9},{9,1},{2,10},{10,2},{3,11},{11,3},{4,12},{12,4},... | collective-permute-start | bytes 811016 | tf_op jit(solution)/shard_map/ppermute | solution.py:226
  11.8 5.5 %collective-permute-start.3 = (f32[2,17,1024]{2,0,1:T(2,128)S(1)}, f32[2,17,1024]{2,0,1:T(2,128)S(1)}, u32[]{:S(2)}, u32[]{:S(2)}) collective-permute-start(f32[2,17,1024]{2,0,1:T(2,128)S(1)} %pad_maximum_fusion.5), channel_id=1, source_target_pairs={{0,2},{1,3},{2,0},{3,1},{4,6},{5,7},{6,4},{7,5},{8,10},{9,11},{10,... | collective-permute-start | bytes 417800 | tf_op jit(solution)/shard_map/ppermute | solution.py:190
  17.6 7.6 %collective-permute-start.4 = (f32[4,17,1024]{2,0,1:T(4,128)S(1)}, f32[4,17,1024]{2,0,1:T(4,128)S(1)}, u32[]{:S(2)}, u32[]{:S(2)}) collective-permute-start(f32[4,17,1024]{2,0,1:T(4,128)S(1)} %pad_maximum_fusion.4), channel_id=1, source_target_pairs={{0,1},{1,0},{2,3},{3,2},{4,5},{5,4},{6,7},{7,6},{8,9},{9,8},{10,11... | collective-permute-start | bytes 835592 | tf_op jit(solution)/shard_map/ppermute | solution.py:190
  26.7 3.5 %collective-permute-start.5 = (f32[8,17,1024]{2,0,1:T(8,128)S(1)}, f32[8,17,1024]{2,0,1:T(8,128)S(1)}, u32[]{:S(2)}, u32[]{:S(2)}) collective-permute-start(f32[8,17,1024]{2,0,1:T(8,128)S(1)} %reshape.170), channel_id=1, source_target_pairs={{0,8},{8,0},{1,9},{9,1},{2,10},{10,2},{3,11},{11,3},{4,12},{12,4},... | collective-permute-start | bytes 1671176 | tf_op jit(solution)/shard_map/ppermute | solution.py:197
  110.5 22.1 %all-to-all-start = ((f32[8,2,1024]{2,1,0:T(2,128)}), f32[8,2,1024]{2,1,0:T(2,128)S(1)}, u32[]{:S(2)}, u32[]{:S(2)}) async-start(f32[8,2,1024]{2,1,0:T(2,128)} %pad_maximum_fusion.6), calls=%async_computation | async-start | bytes 131072 | tf_op jit(solution)/shard_map/all_to_all | solution.py:269
  127.6 5.2 %collective-permute-start.6 = (f32[2048]{0:T(1024)S(1)}, f32[2048]{0:T(1024)S(1)}, u32[]{:S(2)}, u32[]{:S(2)}) collective-permute-start(f32[2048]{0:T(1024)S(1)} %get-tuple-element.9), channel_id=1, source_target_pairs={{0,8},{8,0},{1,9},{9,1},{2,10},{10,2},{3,11},{11,3},{4,12},{12,4},... | collective-permute-start | bytes 24584 | tf_op jit(solution)/shard_map/ppermute | solution.py:267
  132.7 1.2 collective-permute-start.7

commit v3 on v2

--- a/solution.py
+++ b/solution.py
@@ -34,35 +34,41 @@
     return first, second, third
 
 
-def build_table(d, blocks_ref, tab_ref):
+def build_table(d, nbits, blocks_ref, tab_ref):
     scale = 2.0 * LOG2E / epsilon
     slot_row = lax.broadcasted_iota(jnp.int32, (16, BLK), 0)
     used = 3 * d + 16
-
-    def one(tb, carry):
-        blk = blocks_ref[tb]
-        y = blk[0:d, :]
-        yn = jnp.sum(y * y, axis=0, keepdims=True)
-        tp = blk[d:d + 1, :]
-        lt = blk[d + 1:d + 2, :]
-        acol = (lt + (tp - yn) / epsilon) * LOG2E
-        ccol = (-yn / epsilon) * LOG2E
-        y1, y2, y3 = split3_kernel(y * scale)
-        for k, piece in enumerate([y1, y2, y1]):
-            tab_ref[tb, k * d:(k + 1) * d, :] = piece
-        slot = jnp.zeros((16, BLK), jnp.float32)
-        pieces = list(split3_kernel(acol)) + list(split3_kernel(ccol))
-        for k, piece in enumerate(pieces):
-            slot = jnp.where(slot_row == k, piece.astype(jnp.float32), slot)
-        slot = jnp.where((slot_row >= 6) & (slot_row < 9), 1.0, slot)
-        tab_ref[tb, 3 * d:used, :] = slot.astype(jnp.bfloat16)
-        tab_ref[tb, used:KP, :] = jnp.zeros((KP - used, BLK), jnp.bfloat16)
+    per_col = blocks_ref.shape[2] // BLK
+
+    def one(pos, carry):
+        src = 0
+        for i in range(nbits):
+            src = src + ((pos >> i) & 1) * (1 << (nbits - 1 - i))
+        for q in range(per_col):
+            blk = blocks_ref[pos, :, q * BLK:(q + 1) * BLK]
+            tb = src * per_col + q
+            y = blk[0:d, :]
+            yn = jnp.sum(y * y, axis=0, keepdims=True)
+            tp = blk[d:d + 1, :]
+            lt = blk[d + 1:d + 2, :]
+            acol = (lt + (tp - yn) / epsilon) * LOG2E
+            ccol = (-yn / epsilon) * LOG2E
+            y1, y2, y3 = split3_kernel(y * scale)
+            for k, piece in enumerate([y1, y2, y1]):
+                tab_ref[tb, k * d:(k + 1) * d, :] = piece
+            slot = jnp.zeros((16, BLK), jnp.float32)
+            pieces = list(split3_kernel(acol)) + list(split3_kernel(ccol))
+            for k, piece in enumerate(pieces):
+                slot = jnp.where(slot_row == k, piece.astype(jnp.float32), slot)
+            slot = jnp.where((slot_row >= 6) & (slot_row < 9), 1.0, slot)
+            tab_ref[tb, 3 * d:used, :] = slot.astype(jnp.bfloat16)
+            tab_ref[tb, used:KP, :] = jnp.zeros((KP - used, BLK), jnp.bfloat16)
         return carry
 
-    lax.fori_loop(0, tab_ref.shape[0], one, 0)
-
-
-def sinkhorn_kernel(npairs, d, pairs_ref, counts_ref, xt_ref, expand_ref, sel_ref,
+    lax.fori_loop(0, blocks_ref.shape[0], one, 0)
+
+
+def sinkhorn_kernel(npairs, d, nbits, pairs_ref, counts_ref, xt_ref, expand_ref, sel_ref,
                     blocks_ref, fpot_ref, gtop_ref, gsum_ref, sbuf, xr_ref, xc_ref, acc_ref, tab_ref):
     b = pl.program_id(0)
 
@@ -70,7 +76,7 @@
     def _init():
         gtop_ref[...] = jnp.full(gtop_ref.shape, NEG, jnp.float32)
         gsum_ref[...] = jnp.zeros(gsum_ref.shape, jnp.float32)
-        build_table(d, blocks_ref, tab_ref)
+        build_table(d, nbits, blocks_ref, tab_ref)
 
     cnt = counts_ref[b]
     base = b * npairs
@@ -191,17 +197,12 @@
         low = (col_index & step) == 0
         halves = jnp.concatenate(
             [jnp.where(low, halves, partner), jnp.where(low, partner, halves)], axis=0)
-    halves = jnp.transpose(
-        halves.reshape((2,) * nbits + (share, own_targets)),
-        tuple(reversed(range(nbits))) + (nbits, nbits + 1)).reshape(ncols, share, own_targets)
     other = lax.ppermute(halves, "rows", [(0, 1), (1, 0)])
     first = lax.axis_index("rows") == 0
     gathered = jnp.concatenate(
         [jnp.where(first, halves, other), jnp.where(first, other, halves)], axis=1)
     nt = ncols * own_targets
     tblocks = nt // BLK
-    blocks = jnp.transpose(
-        gathered.reshape(ncols, rowsp, own_targets // BLK, BLK), (0, 2, 1, 3)).reshape(tblocks, rowsp, BLK)
 
     col = jnp.arange(KP, dtype=jnp.int32)[None, :]
     comp = jnp.arange(d, dtype=jnp.int32)[:, None]
@@ -238,7 +239,7 @@
             pl.BlockSpec((BLK, d + 1), lambda b, pr, ct: (b, 0)),
             pl.BlockSpec((3, d, KP), lambda b, pr, ct: (0, 0, 0)),
             pl.BlockSpec((8, KP), lambda b, pr, ct: (0, 0)),
-            pl.BlockSpec((tblocks, rowsp, BLK), lambda b, pr, ct: (0, 0, 0)),
+            pl.BlockSpec((ncols, rowsp, own_targets), lambda b, pr, ct: (0, 0, 0)),
         ],
         out_specs=[
             pl.BlockSpec((BLK, 1), lambda b, pr, ct: (b, 0)),
@@ -252,7 +253,7 @@
                         pltpu.VMEM((tblocks, KP, BLK), jnp.bfloat16)],
     )
     fpot, gtop, gsum = pl.pallas_call(
-        functools.partial(sinkhorn_kernel, npairs, d),
+        functools.partial(sinkhorn_kernel, npairs, d, nbits),
         grid_spec=grid_spec,
         out_shape=[
             jax.ShapeDtypeStruct((ns, 1), jnp.float32),
@@ -261,7 +262,7 @@
         ],
         compiler_params=pltpu.CompilerParams(
             dimension_semantics=("arbitrary",), vmem_limit_bytes=100 * 1024 * 1024),
-    )(pairs.reshape(-1), counts, xt, expand, sel, blocks)
+    )(pairs.reshape(-1), counts, xt, expand, sel, gathered)
 
     done = fpot.reshape(-1)
     src_pot = jnp.concatenate([done[:kept], lax.ppermute(done[kept:], "rows", swap)])

time: 133 us -> 134 us (level)
  waiting for transfers between devices: 17.2 us -> 22 us
  Pallas kernels: 77 us -> 72.6 us
  local copies, waits for them, and re-layouts: 8.39 us -> 6.05 us
    ppermute x3, waiting for transfers between devices: 12.4 us -> 17.2 us  [on_device(): lax.ppermute(halves, 'cols', [(i, i ^ step) for i in range(ncols)])]
    pallas_call x1, Pallas kernels: 77 us -> 72.6 us  [on_device(): pl.pallas_call(functools.partial(sinkhorn_kernel, npairs, d, nbits), grid...]
    reshape x3 -> x0, local copies, waits for them, and re-layouts: 1.9 us -> none  [the longest x1 1.19 us: on_device(): blocks = jnp.transpose(gathered.reshape(ncols, rowsp, own_targets // BLK,...]
  transfers between devices with their start and end apart: 9 -> 9, of which waited for: 5 -> 5; matrix products, arithmetic and copies ran while one was open for 9% -> 8% of each run, Pallas kernels for 0% -> 0%
where the time goes in v3:
time: 134 us; the launch traced here: 135 us
  Pallas kernels  72.6 us (54%)
  starting transfers between devices  23.4 us (17%)
  waiting for transfers between devices  22 us (16%)
  other arithmetic  9.83 us (7%)
  local copies, waits for them, and re-layouts  6.05 us (5%)
    pallas_call x1, Pallas kernels, on_device(): pl.pallas_call(functools.partial(sinkhorn_kernel, npairs, d, nbits), grid...  72.6 us
    ppermute x3, waiting for transfers between devices, on_device(): lax.ppermute(halves, 'cols', [(i, i ^ step) for i in range(ncols)])  17.2 us
    all_to_all x1, starting transfers between devices, on_device(): mine = lax.all_to_all(parts, 'cols', 0, 0, tiled=True)  16.2 us
    ppermute x3, starting transfers between devices, on_device(): lax.ppermute(halves, 'cols', [(i, i ^ step) for i in range(ncols)])  5.93 us
    all_to_all x1, waiting for transfers between devices, on_device(): mine = lax.all_to_all(parts, 'cols', 0, 0, tiled=True)  4.26 us
  transfers between devices with their start and end apart: 9, of which 5 were waited for; matrix products, arithmetic and copies ran while one was open for 8% of the time, Pallas kernels for 0%

profile of v3, /device:TPU:0, one launch (start us, length us, event | category | flops | bytes accessed | tf_op | source)
XLA Modules:
  0.0 134.7 jit_solution(4284849932875946493)
XLA Ops:
  0.6 0.0 copy-start
  0.6 0.0 copy-start.2
  0.7 0.0 copy-start.1
  0.7 0.8 copy.25
  1.5 0.8 fusion.19
  2.2 0.5 collective-permute-start
  2.7 1.0 fusion.3
  3.7 3.7 %collective-permute-start.2 = (f32[1,17,1024]{2,1,0:T(8,128)S(1)}, f32[1,17,1024]{2,1,0:T(8,128)S(1)}, u32[]{:S(2)}, u32[]{:S(2)}) collective-permute-start(f32[1,17,1024]{2,1,0:T(8,128)S(1)} %fusion.3), channel_id=1, source_target_pairs={{0,4},{1,5},{2,6},{3,7},{4,0},{5,1},{6,2},{7,3},{8,12},{9,13},{10,... | collective-permute-start | bytes 208904 | tf_op jit(solution)/shard_map/ppermute | solution.py:196
  7.3 1.1 fusion
  8.4 0.2 collective-permute-start.1
  8.7 0.1 fusion.10
  8.7 4.1 %collective-permute-done.2 = f32[1,17,1024]{2,1,0:T(8,128)S(1)} collective-permute-done((f32[1,17,1024]{2,1,0:T(8,128)S(1)}, f32[1,17,1024]{2,1,0:T(8,128)S(1)}, u32[]{:S(2)}, u32[]{:S(2)}) %collective-permute-start.2) | collective-permute-done | bytes 69664 | tf_op jit(solution)/shard_map/ppermute | solution.py:196
  12.8 0.0 copy-done
  12.8 0.0 copy-done.2
  12.8 0.0 copy-done.1
  12.8 0.1 broadcast_select_fusion.5
  12.9 0.8 collective-permute-start.3
  13.8 5.9 %collective-permute-done.3 = f32[2,17,1024]{2,1,0:T(8,128)S(1)} collective-permute-done((f32[2,17,1024]{2,1,0:T(8,128)S(1)}, f32[2,17,1024]{2,1,0:T(8,128)S(1)}, u32[]{:S(2)}, u32[]{:S(2)}) %collective-permute-start.3) | collective-permute-done | bytes 139296 | tf_op jit(solution)/shard_map/ppermute | solution.py:196
  19.7 1.4 %collective-permute-start.4 = (f32[4,17,1024]{2,1,0:T(8,128)S(1)}, f32[4,17,1024]{2,1,0:T(8,128)S(1)}, u32[]{:S(2)}, u32[]{:S(2)}) collective-permute-start(f32[4,17,1024]{2,1,0:T(8,128)S(1)} %pad_maximum_fusion.3), channel_id=1, source_target_pairs={{0,1},{1,0},{2,3},{3,2},{4,5},{5,4},{6,7},{7,6},{8,9},{9,8},{10,11... | collective-permute-start | bytes 835592 | tf_op jit(solution)/shard_map/ppermute | solution.py:196
  21.2 0.6 convert_element_type.25.sel_ref
  21.8 0.1 pad.21.clone
  21.9 0.7 maximum_maximum_fusion.expand_ref
  22.6 7.2 %collective-permute-done.4 = f32[4,17,1024]{2,1,0:T(8,128)S(1)} collective-permute-done((f32[4,17,1024]{2,1,0:T(8,128)S(1)}, f32[4,17,1024]{2,1,0:T(8,128)S(1)}, u32[]{:S(2)}, u32[]{:S(2)}) %collective-permute-start.4) | collective-permute-done | bytes 278560 | tf_op jit(solution)/shard_map/ppermute | solution.py:196
  29.8 0.1 broadcast_select_fusion.1
  29.9 0.1 pad_maximum_fusion.1
  29.9 0.3 copy.27
  30.3 0.1 collective-permute-start.5
  30.4 0.0 collective-permute-done
  30.4 0.7 reshape.158.pairs_ref
  31.0 0.8 fusion.16.counts_ref
  31.8 0.0 collective-permute-done.1
  31.9 2.0 %copy.26 = f32[33,4096]{0,1:T(8,128)} copy(f32[33,4096]{1,0:T(8,128)S(1)} %pad_maximum_fusion.2) | data formatting | bytes 1081344 | tf_op jit(solution)/shard_map/concatenate | solution.py:227
  33.8 0.0 collective-permute-done.5
  33.8 0.4 copy_select_fusion.1
  34.2 1.2 pad_maximum_fusion.blocks_ref
  35.5 72.6 %shard_map.86 = (f32[4096,1]{1,0:T(8,128)}, f32[32,1,256]{2,1,0:T(1,128)}, f32[32,1,256]{2,1,0:T(1,128)}) custom-call(s32[384]{0:T(512)} %reshape.158.pairs_ref, s32[16]{0:T(128)} %fusion.16.counts_ref, f32[4096,33]{1,0:T(8,128)} %bitcast.44, bf16[3,32,128]{2,1,0:T(8,128)(2,1)} %maximum_maximum_fusion.expand_ref, f32[8,128]{1,0:T(8,128)} %convert_element_type.25.sel_ref, ...), custom_call_target="tpu_custom_call" | custom-call | tf_op jit(solution)/shard_map/pallas_call | solution.py:255
  108.0 1.5 %pad_maximum_fusion.6 = f32[8,2,1024]{2,1,0:T(2,128)} fusion(f32[8,1,1024]{2,1,0:T(1,128)} %bitcast.50, f32[8,1,1024]{2,1,0:T(1,128)} %bitcast.49), kind=kLoop, calls=%fused_computation.23 | loop fusion | flops 16384 | bytes 131072 | tf_op jit(solution)/shard_map/stack | solution.py:269
  109.5 16.2 %all-to-all-start = ((f32[8,2,1024]{2,1,0:T(2,128)}), f32[8,2,1024]{2,1,0:T(2,128)S(1)}, u32[]{:S(2)}, u32[]{:S(2)}) async-start(f32[8,2,1024]{2,1,0:T(2,128)} %pad_maximum_fusion.6), calls=%async_computation | async-start | bytes 131072 | tf_op jit(solution)/shard_map/all_to_all | solution.py:270
  125.7 2.1 %slice_reduce_fusion.1 = (f32[2048]{0:T(1024)S(1)}, f32[2048]{0:T(1024)S(1)}) fusion(f32[4096,1]{1,0:T(8,128)} %get-tuple-element.5), kind=kLoop, calls=%fused_computation.2 | loop fusion | bytes 32768 | tf_op jit(solution)/shard_map/slice | solution.py:268
  127.8 0.5 collective-permute-start.6
  128.3 4.3 %all-to-all-done = f32[8,2,1024]{2,1,0:T(2,128)S(1)} async-done(((f32[8,2,1024]{2,1,0:T(2,128)}), f32[8,2,1024]{2,1,0:T(2,128)S(1)}, u32[]{:S(2)}, u32[]{:S(2)}) %all-to-all-start) | async-done | bytes 65568 | tf_op jit(solution)/shard_map/all_to_all | solution.py:270
  132.6 0.1 slice_reduce_fusion.2
  132.7 0.1 collective-permute-start.7
  132.8 0.0 collective-permute-done.6
  132.8 0.6 pad_maximum_fusion.7
  133.4 0.5 collective-permute-done.7
  134.1 0.6 add_multiply_fusion
  (19 shorter events, 0.3 us)
Async XLA Ops:
  0.6 12.2 %copy-start = (f32[32,1024]{1,0:T(8,128)S(1)}, f32[32,1024]{1,0:T(8,128)}, u32[]{:S(2)}) copy-start(f32[32,1024]{1,0:T(8,128)} %param.8) | copy-start | bytes 393220
  0.6 12.2 %copy-start.2 = (f32[1024]{0:T(1024)S(1)}, f32[1024]{0:T(1024)}, u32[]{:S(2)}) copy-start(f32[1024]{0:T(1024)} %param.11) | copy-start | bytes 12292
  0.7 12.2 %copy-start.1 = (f32[1024]{0:T(1024)S(1)}, f32[1024]{0:T(1024)}, u32[]{:S(2)}) copy-start(f32[1024]{0:T(1024)} %param.9) | copy-start | bytes 12292
  2.2 28.1 %collective-permute-start = (s32[8,25]{1,0:T(8,128)S(1)}, s32[8,25]{1,0:T(8,128)S(1)}, u32[]{:S(2)}, u32[]{:S(2)}) collective-permute-start(s32[8,25]{1,0:T(8,128)S(1)} %get-tuple-element.28), channel_id=1, source_target_pairs={{0,8},{8,0},{1,9},{9,1},{2,10},{10,2},{3,11},{11,3},{4,12},{12,4},... | collective-permute-start | bytes 2408 | tf_op jit(solution)/shard_map/ppermute | solution.py:229
  3.7 9.2 %collective-permute-start.2 = (f32[1,17,1024]{2,1,0:T(8,128)S(1)}, f32[1,17,1024]{2,1,0:T(8,128)S(1)}, u32[]{:S(2)}, u32[]{:S(2)}) collective-permute-start(f32[1,17,1024]{2,1,0:T(8,128)S(1)} %fusion.3), channel_id=1, source_target_pairs={{0,4},{1,5},{2,6},{3,7},{4,0},{5,1},{6,2},{7,3},{8,12},{9,13},{10,... | collective-permute-start | bytes 208904 | tf_op jit(solution)/shard_map/ppermute | solution.py:196
  8.4 23.4 %collective-permute-start.1 = (f32[33,2048]{1,0:T(8,128)S(1)}, f32[33,2048]{1,0:T(8,128)S(1)}, u32[]{:S(2)}, u32[]{:S(2)}) collective-permute-start(f32[33,2048]{1,0:T(8,128)S(1)} %get-tuple-element.17), channel_id=1, source_target_pairs={{0,8},{8,0},{1,9},{9,1},{2,10},{10,2},{3,11},{11,3},{4,12},{12,4},... | collective-permute-start | bytes 811016 | tf_op jit(solution)/shard_map/ppermute | solution.py:227
  12.9 6.7 %collective-permute-start.3 = (f32[2,17,1024]{2,1,0:T(8,128)S(1)}, f32[2,17,1024]{2,1,0:T(8,128)S(1)}, u32[]{:S(2)}, u32[]{:S(2)}) collective-permute-start(f32[2,17,1024]{2,1,0:T(8,128)S(1)} %pad_maximum_fusion.5), channel_id=1, source_target_pairs={{0,2},{1,3},{2,0},{3,1},{4,6},{5,7},{6,4},{7,5},{8,10},{9,11},{10,... | collective-permute-start | bytes 417800 | tf_op jit(solution)/shard_map/ppermute | solution.py:196
  19.7 10.1 %collective-permute-start.4 = (f32[4,17,1024]{2,1,0:T(8,128)S(1)}, f32[4,17,1024]{2,1,0:T(8,128)S(1)}, u32[]{:S(2)}, u32[]{:S(2)}) collective-permute-start(f32[4,17,1024]{2,1,0:T(8,128)S(1)} %pad_maximum_fusion.3), channel_id=1, source_target_pairs={{0,1},{1,0},{2,3},{3,2},{4,5},{5,4},{6,7},{7,6},{8,9},{9,8},{10,11... | collective-permute-start | bytes 835592 | tf_op jit(solution)/shard_map/ppermute | solution.py:196
  30.3 3.6 %collective-permute-start.5 = (f32[8,17,1024]{2,0,1:T(8,128)S(1)}, f32[8,17,1024]{2,0,1:T(8,128)S(1)}, u32[]{:S(2)}, u32[]{:S(2)}) collective-permute-start(f32[8,17,1024]{2,0,1:T(8,128)S(1)} %copy.27), channel_id=1, source_target_pairs={{0,8},{8,0},{1,9},{9,1},{2,10},{10,2},{3,11},{11,3},{4,12},{12,4},... | collective-permute-start | bytes 1671176 | tf_op jit(solution)/shard_map/ppermute | solution.py:200
  109.5 23.1 %all-to-all-start = ((f32[8,2,1024]{2,1,0:T(2,128)}), f32[8,2,1024]{2,1,0:T(2,128)S(1)}, u32[]{:S(2)}, u32[]{:S(2)}) async-start(f32[8,2,1024]{2,1,0:T(2,128)} %pad_maximum_fusion.6), calls=%async_computation | async-start | bytes 131072 | tf_op jit(solution)/shard_map/all_to_all | solution.py:270
  127.8 5.0 %collective-permute-start.6 = (f32[2048]{0:T(1024)S(1)}, f32[2048]{0:T(1024)S(1)}, u32[]{:S(2)}, u32[]{:S(2)}) collective-permute-start(f32[2048]{0:T(1024)S(1)} %get-tuple-element.9), channel_id=1, source_target_pairs={{0,8},{8,0},{1,9},{9,1},{2,10},{10,2},{3,11},{11,3},{4,12},{12,4},... | collective-permute-start | bytes 24584 | tf_op jit(solution)/shard_map/ppermute | solution.py:268
  132.7 1.2 collective-permute-start.7

commit v4 on v3

--- a/solution.py
+++ b/solution.py
@@ -166,7 +166,30 @@
             gsum_ref[tb] = gsum_ref[tb] * jnp.exp2(old - new) + cs * jnp.exp2(cm - new)
             gtop_ref[tb] = new
 
-    quads_of(col_pass)
+    def octets_of(body):
+        def eight(k, carry):
+            body([8 * k + i for i in range(8)])
+            return carry
+
+        lax.fori_loop(0, cnt // 8, eight, 0)
+        rest = cnt % 8
+        start4 = cnt - rest
+
+        @pl.when(rest >= 4)
+        def _four():
+            body([start4 + i for i in range(4)])
+
+        start2 = start4 + (rest // 4) * 4
+
+        @pl.when(rest % 4 >= 2)
+        def _pair():
+            body([start2, start2 + 1])
+
+        @pl.when(cnt % 2 == 1)
+        def _last():
+            body([cnt - 1])
+
+    octets_of(col_pass)
 
 
 def merge(tops, sums, axis):
@@ -246,7 +269,7 @@
             pl.BlockSpec((tblocks, 1, BLK), lambda b, pr, ct: (0, 0, 0)),
             pl.BlockSpec((tblocks, 1, BLK), lambda b, pr, ct: (0, 0, 0)),
         ],
-        scratch_shapes=[pltpu.VMEM((4, BLK, BLK), jnp.float32),
+        scratch_shapes=[pltpu.VMEM((8, BLK, BLK), jnp.float32),
                         pltpu.VMEM((BLK, KP), jnp.bfloat16),
                         pltpu.VMEM((BLK, KP), jnp.bfloat16),
                         pltpu.VMEM((4, BLK, LANE), jnp.float32),

time: 134 us -> 127 us (0.948); the launches traced: 135 us -> 124 us
  starting transfers between devices: 23.4 us -> 17.2 us
  Pallas kernels: 72.6 us -> 67.9 us
    all_to_all x1, starting transfers between devices: 16.2 us -> 10.4 us  [on_device(): mine = lax.all_to_all(parts, 'cols', 0, 0, tiled=True)]
    pallas_call x1, Pallas kernels: 72.6 us -> 67.9 us  [on_device(): pl.pallas_call(functools.partial(sinkhorn_kernel, npairs, d, nbits), grid...]
where the time goes in v4:
time: 127 us; the launch traced here: 124 us
  Pallas kernels  67.9 us (53%)
  waiting for transfers between devices  22.4 us (18%)
  starting transfers between devices  17.2 us (14%)
  other arithmetic  9.83 us (8%)
  local copies, waits for them, and re-layouts  6.05 us (5%)
    pallas_call x1, Pallas kernels, on_device(): pl.pallas_call(functools.partial(sinkhorn_kernel, npairs, d, nbits), grid...  67.9 us
    ppermute x3, waiting for transfers between devices, on_device(): lax.ppermute(halves, 'cols', [(i, i ^ step) for i in range(ncols)])  17.2 us
    all_to_all x1, starting transfers between devices, on_device(): mine = lax.all_to_all(parts, 'cols', 0, 0, tiled=True)  10.4 us
    ppermute x3, starting transfers between devices, on_device(): lax.ppermute(halves, 'cols', [(i, i ^ step) for i in range(ncols)])  5.93 us
    all_to_all x1, waiting for transfers between devices, on_device(): mine = lax.all_to_all(parts, 'cols', 0, 0, tiled=True)  4.67 us
  transfers between devices with their start and end apart: 9, of which 5 were waited for; matrix products, arithmetic and copies ran while one was open for 8% of the time, Pallas kernels for 0%

profile of v4, /device:TPU:0, one launch (start us, length us, event | category | flops | bytes accessed | tf_op | source)
XLA Modules:
  0.0 124.2 jit_solution(13312462292027299276)
XLA Ops:
  0.6 0.0 copy-start
  0.6 0.0 copy-start.2
  0.7 0.0 copy-start.1
  0.7 0.8 copy.25
  1.5 0.8 fusion.19
  2.2 0.5 collective-permute-start
  2.7 1.0 fusion.3
  3.7 3.7 %collective-permute-start.2 = (f32[1,17,1024]{2,1,0:T(8,128)S(1)}, f32[1,17,1024]{2,1,0:T(8,128)S(1)}, u32[]{:S(2)}, u32[]{:S(2)}) collective-permute-start(f32[1,17,1024]{2,1,0:T(8,128)S(1)} %fusion.3), channel_id=1, source_target_pairs={{0,4},{1,5},{2,6},{3,7},{4,0},{5,1},{6,2},{7,3},{8,12},{9,13},{10,... | collective-permute-start | bytes 208904 | tf_op jit(solution)/shard_map/ppermute | solution.py:219
  7.3 1.1 fusion
  8.4 0.2 collective-permute-start.1
  8.7 0.1 fusion.10
  8.7 4.1 %collective-permute-done.2 = f32[1,17,1024]{2,1,0:T(8,128)S(1)} collective-permute-done((f32[1,17,1024]{2,1,0:T(8,128)S(1)}, f32[1,17,1024]{2,1,0:T(8,128)S(1)}, u32[]{:S(2)}, u32[]{:S(2)}) %collective-permute-start.2) | collective-permute-done | bytes 69664 | tf_op jit(solution)/shard_map/ppermute | solution.py:219
  12.8 0.0 copy-done
  12.8 0.0 copy-done.2
  12.8 0.0 copy-done.1
  12.8 0.1 broadcast_select_fusion.5
  12.9 0.8 collective-permute-start.3
  13.8 5.9 %collective-permute-done.3 = f32[2,17,1024]{2,1,0:T(8,128)S(1)} collective-permute-done((f32[2,17,1024]{2,1,0:T(8,128)S(1)}, f32[2,17,1024]{2,1,0:T(8,128)S(1)}, u32[]{:S(2)}, u32[]{:S(2)}) %collective-permute-start.3) | collective-permute-done | bytes 139296 | tf_op jit(solution)/shard_map/ppermute | solution.py:219
  19.7 1.4 %collective-permute-start.4 = (f32[4,17,1024]{2,1,0:T(8,128)S(1)}, f32[4,17,1024]{2,1,0:T(8,128)S(1)}, u32[]{:S(2)}, u32[]{:S(2)}) collective-permute-start(f32[4,17,1024]{2,1,0:T(8,128)S(1)} %pad_maximum_fusion.3), channel_id=1, source_target_pairs={{0,1},{1,0},{2,3},{3,2},{4,5},{5,4},{6,7},{7,6},{8,9},{9,8},{10,11... | collective-permute-start | bytes 835592 | tf_op jit(solution)/shard_map/ppermute | solution.py:219
  21.2 0.6 convert_element_type.25.sel_ref
  21.8 0.1 pad.21.clone
  21.9 0.7 maximum_maximum_fusion.expand_ref
  22.6 7.2 %collective-permute-done.4 = f32[4,17,1024]{2,1,0:T(8,128)S(1)} collective-permute-done((f32[4,17,1024]{2,1,0:T(8,128)S(1)}, f32[4,17,1024]{2,1,0:T(8,128)S(1)}, u32[]{:S(2)}, u32[]{:S(2)}) %collective-permute-start.4) | collective-permute-done | bytes 278560 | tf_op jit(solution)/shard_map/ppermute | solution.py:219
  29.8 0.1 broadcast_select_fusion.1
  29.9 0.1 pad_maximum_fusion.1
  29.9 0.3 copy.27
  30.3 0.1 collective-permute-start.5
  30.4 0.0 collective-permute-done
  30.4 0.7 reshape.158.pairs_ref
  31.0 0.8 fusion.16.counts_ref
  31.8 0.0 collective-permute-done.1
  31.9 2.0 %copy.26 = f32[33,4096]{0,1:T(8,128)} copy(f32[33,4096]{1,0:T(8,128)S(1)} %pad_maximum_fusion.2) | data formatting | bytes 1081344 | tf_op jit(solution)/shard_map/concatenate | solution.py:250
  33.8 0.0 collective-permute-done.5
  33.8 0.4 copy_select_fusion.1
  34.2 1.2 %pad_maximum_fusion.blocks_ref = f32[8,34,1024]{2,1,0:T(8,128)} fusion(f32[8,17,1024]{2,1,0:T(8,128)S(1)} %get-tuple-element.13, f32[8,17,1024]{2,1,0:T(8,128)S(1)} %get-tuple-element.12), kind=kLoop, calls=%fused_computation | loop fusion | flops 278528 | bytes 2228224 | tf_op jit(solution)/shard_map/concatenate | solution.py:225
  35.5 67.9 %shard_map.86 = (f32[4096,1]{1,0:T(8,128)}, f32[32,1,256]{2,1,0:T(1,128)}, f32[32,1,256]{2,1,0:T(1,128)}) custom-call(s32[384]{0:T(512)} %reshape.158.pairs_ref, s32[16]{0:T(128)} %fusion.16.counts_ref, f32[4096,33]{1,0:T(8,128)} %bitcast.44, bf16[3,32,128]{2,1,0:T(8,128)(2,1)} %maximum_maximum_fusion.expand_ref, f32[8,128]{1,0:T(8,128)} %convert_element_type.25.sel_ref, ...), custom_call_target="tpu_custom_call" | custom-call | tf_op jit(solution)/shard_map/pallas_call | solution.py:278
  103.4 1.5 %pad_maximum_fusion.6 = f32[8,2,1024]{2,1,0:T(2,128)} fusion(f32[8,1,1024]{2,1,0:T(1,128)} %bitcast.50, f32[8,1,1024]{2,1,0:T(1,128)} %bitcast.49), kind=kLoop, calls=%fused_computation.23 | loop fusion | flops 16384 | bytes 131072 | tf_op jit(solution)/shard_map/stack | solution.py:292
  104.8 10.4 %all-to-all-start = ((f32[8,2,1024]{2,1,0:T(2,128)}), f32[8,2,1024]{2,1,0:T(2,128)S(1)}, u32[]{:S(2)}, u32[]{:S(2)}) async-start(f32[8,2,1024]{2,1,0:T(2,128)} %pad_maximum_fusion.6), calls=%async_computation | async-start | bytes 131072 | tf_op jit(solution)/shard_map/all_to_all | solution.py:293
  115.2 2.1 %slice_reduce_fusion.1 = (f32[2048]{0:T(1024)S(1)}, f32[2048]{0:T(1024)S(1)}) fusion(f32[4096,1]{1,0:T(8,128)} %get-tuple-element.5), kind=kLoop, calls=%fused_computation.2 | loop fusion | bytes 32768 | tf_op jit(solution)/shard_map/slice | solution.py:291
  117.4 0.1 collective-permute-start.6
  117.4 4.7 %all-to-all-done = f32[8,2,1024]{2,1,0:T(2,128)S(1)} async-done(((f32[8,2,1024]{2,1,0:T(2,128)}), f32[8,2,1024]{2,1,0:T(2,128)S(1)}, u32[]{:S(2)}, u32[]{:S(2)}) %all-to-all-start) | async-done | bytes 65568 | tf_op jit(solution)/shard_map/all_to_all | solution.py:293
  122.1 0.1 slice_reduce_fusion.2
  122.2 0.1 collective-permute-start.7
  122.3 0.0 collective-permute-done.6
  122.3 0.6 pad_maximum_fusion.7
  122.9 0.5 collective-permute-done.7
  123.6 0.6 add_multiply_fusion
  (19 shorter events, 0.3 us)
Async XLA Ops:
  0.6 12.2 %copy-start = (f32[32,1024]{1,0:T(8,128)S(1)}, f32[32,1024]{1,0:T(8,128)}, u32[]{:S(2)}) copy-start(f32[32,1024]{1,0:T(8,128)} %param.8) | copy-start | bytes 393220
  0.6 12.2 %copy-start.2 = (f32[1024]{0:T(1024)S(1)}, f32[1024]{0:T(1024)}, u32[]{:S(2)}) copy-start(f32[1024]{0:T(1024)} %param.11) | copy-start | bytes 12292
  0.7 12.2 %copy-start.1 = (f32[1024]{0:T(1024)S(1)}, f32[1024]{0:T(1024)}, u32[]{:S(2)}) copy-start(f32[1024]{0:T(1024)} %param.9) | copy-start | bytes 12292
  2.2 28.1 %collective-permute-start = (s32[8,25]{1,0:T(8,128)S(1)}, s32[8,25]{1,0:T(8,128)S(1)}, u32[]{:S(2)}, u32[]{:S(2)}) collective-permute-start(s32[8,25]{1,0:T(8,128)S(1)} %get-tuple-element.28), channel_id=1, source_target_pairs={{0,8},{8,0},{1,9},{9,1},{2,10},{10,2},{3,11},{11,3},{4,12},{12,4},... | collective-permute-start | bytes 2408 | tf_op jit(solution)/shard_map/ppermute | solution.py:252
  3.7 9.2 %collective-permute-start.2 = (f32[1,17,1024]{2,1,0:T(8,128)S(1)}, f32[1,17,1024]{2,1,0:T(8,128)S(1)}, u32[]{:S(2)}, u32[]{:S(2)}) collective-permute-start(f32[1,17,1024]{2,1,0:T(8,128)S(1)} %fusion.3), channel_id=1, source_target_pairs={{0,4},{1,5},{2,6},{3,7},{4,0},{5,1},{6,2},{7,3},{8,12},{9,13},{10,... | collective-permute-start | bytes 208904 | tf_op jit(solution)/shard_map/ppermute | solution.py:219
  8.4 23.4 %collective-permute-start.1 = (f32[33,2048]{1,0:T(8,128)S(1)}, f32[33,2048]{1,0:T(8,128)S(1)}, u32[]{:S(2)}, u32[]{:S(2)}) collective-permute-start(f32[33,2048]{1,0:T(8,128)S(1)} %get-tuple-element.17), channel_id=1, source_target_pairs={{0,8},{8,0},{1,9},{9,1},{2,10},{10,2},{3,11},{11,3},{4,12},{12,4},... | collective-permute-start | bytes 811016 | tf_op jit(solution)/shard_map/ppermute | solution.py:250
  12.9 6.7 %collective-permute-start.3 = (f32[2,17,1024]{2,1,0:T(8,128)S(1)}, f32[2,17,1024]{2,1,0:T(8,128)S(1)}, u32[]{:S(2)}, u32[]{:S(2)}) collective-permute-start(f32[2,17,1024]{2,1,0:T(8,128)S(1)} %pad_maximum_fusion.5), channel_id=1, source_target_pairs={{0,2},{1,3},{2,0},{3,1},{4,6},{5,7},{6,4},{7,5},{8,10},{9,11},{10,... | collective-permute-start | bytes 417800 | tf_op jit(solution)/shard_map/ppermute | solution.py:219
  19.7 10.1 %collective-permute-start.4 = (f32[4,17,1024]{2,1,0:T(8,128)S(1)}, f32[4,17,1024]{2,1,0:T(8,128)S(1)}, u32[]{:S(2)}, u32[]{:S(2)}) collective-permute-start(f32[4,17,1024]{2,1,0:T(8,128)S(1)} %pad_maximum_fusion.3), channel_id=1, source_target_pairs={{0,1},{1,0},{2,3},{3,2},{4,5},{5,4},{6,7},{7,6},{8,9},{9,8},{10,11... | collective-permute-start | bytes 835592 | tf_op jit(solution)/shard_map/ppermute | solution.py:219
  30.3 3.6 %collective-permute-start.5 = (f32[8,17,1024]{2,0,1:T(8,128)S(1)}, f32[8,17,1024]{2,0,1:T(8,128)S(1)}, u32[]{:S(2)}, u32[]{:S(2)}) collective-permute-start(f32[8,17,1024]{2,0,1:T(8,128)S(1)} %copy.27), channel_id=1, source_target_pairs={{0,8},{8,0},{1,9},{9,1},{2,10},{10,2},{3,11},{11,3},{4,12},{12,4},... | collective-permute-start | bytes 1671176 | tf_op jit(solution)/shard_map/ppermute | solution.py:223
  104.8 17.3 %all-to-all-start = ((f32[8,2,1024]{2,1,0:T(2,128)}), f32[8,2,1024]{2,1,0:T(2,128)S(1)}, u32[]{:S(2)}, u32[]{:S(2)}) async-start(f32[8,2,1024]{2,1,0:T(2,128)} %pad_maximum_fusion.6), calls=%async_computation | async-start | bytes 131072 | tf_op jit(solution)/shard_map/all_to_all | solution.py:293
  117.4 5.0 %collective-permute-start.6 = (f32[2048]{0:T(1024)S(1)}, f32[2048]{0:T(1024)S(1)}, u32[]{:S(2)}, u32[]{:S(2)}) collective-permute-start(f32[2048]{0:T(1024)S(1)} %get-tuple-element.9), channel_id=1, source_target_pairs={{0,8},{8,0},{1,9},{9,1},{2,10},{10,2},{3,11},{11,3},{4,12},{12,4},... | collective-permute-start | bytes 24584 | tf_op jit(solution)/shard_map/ppermute | solution.py:291
  122.2 1.2 collective-permute-start.7

commit v5 on v4

--- a/solution.py
+++ b/solution.py
@@ -90,7 +90,7 @@
           + jnp.dot(x3, expand_ref[2], preferred_element_type=jnp.float32))
     sel = sel_ref[...]
     xr_ref[...] = (xa + sel[0:1, :]).astype(jnp.bfloat16)
-    for a in range(2):
+    for a in range(4):
         acc_ref[2 * a] = jnp.full((BLK, LANE), NEG, jnp.float32)
         acc_ref[2 * a + 1] = jnp.zeros((BLK, LANE), jnp.float32)
 
@@ -137,22 +137,8 @@
         acc_ref[2 * a + 1] = total
 
     def row_pass(ts):
-        row_update(ts[:2], 0)
-        if len(ts) > 2:
-            row_update(ts[2:], 1)
-
-    quads_of(row_pass)
-    top_a = acc_ref[0]
-    top_b = acc_ref[2]
-    lane_top = jnp.maximum(top_a, top_b)
-    m = jnp.max(lane_top, axis=1, keepdims=True)
-    lane_sum = (acc_ref[1] * jnp.exp2(top_a - m) + acc_ref[3] * jnp.exp2(top_b - m))
-    lse = m + jnp.log2(jnp.sum(lane_sum, axis=1, keepdims=True))
-    fpot_ref[...] = xn - (epsilon * LN2) * lse
-    p1, p2, p3 = split3_kernel(ls * LOG2E - lse)
-    xc_ref[...] = (xa + sel[1:2, :] + p1.astype(jnp.float32) * sel[2:3, :]
-                   + p2.astype(jnp.float32) * sel[3:4, :]
-                   + p3.astype(jnp.float32) * sel[4:5, :]).astype(jnp.bfloat16)
+        for a in range(0, len(ts), 2):
+            row_update(ts[a:a + 2], a // 2)
 
     def col_pass(ts):
         for slot, t in enumerate(ts):
@@ -188,6 +174,22 @@
         @pl.when(cnt % 2 == 1)
         def _last():
             body([cnt - 1])
+
+    octets_of(row_pass)
+    tops = [acc_ref[2 * a] for a in range(4)]
+    lane_top = tops[0]
+    for t in tops[1:]:
+        lane_top = jnp.maximum(lane_top, t)
+    m = jnp.max(lane_top, axis=1, keepdims=True)
+    lane_sum = acc_ref[1] * jnp.exp2(tops[0] - m)
+    for a in range(1, 4):
+        lane_sum = lane_sum + acc_ref[2 * a + 1] * jnp.exp2(tops[a] - m)
+    lse = m + jnp.log2(jnp.sum(lane_sum, axis=1, keepdims=True))
+    fpot_ref[...] = xn - (epsilon * LN2) * lse
+    p1, p2, p3 = split3_kernel(ls * LOG2E - lse)
+    xc_ref[...] = (xa + sel[1:2, :] + p1.astype(jnp.float32) * sel[2:3, :]
+                   + p2.astype(jnp.float32) * sel[3:4, :]
+                   + p3.astype(jnp.float32) * sel[4:5, :]).astype(jnp.bfloat16)
 
     octets_of(col_pass)
 
@@ -272,7 +274,7 @@
         scratch_shapes=[pltpu.VMEM((8, BLK, BLK), jnp.float32),
                         pltpu.VMEM((BLK, KP), jnp.bfloat16),
                         pltpu.VMEM((BLK, KP), jnp.bfloat16),
-                        pltpu.VMEM((4, BLK, LANE), jnp.float32),
+                        pltpu.VMEM((8, BLK, LANE), jnp.float32),
                         pltpu.VMEM((tblocks, KP, BLK), jnp.bfloat16)],
     )
     fpot, gtop, gsum = pl.pallas_call(

time: 127 us -> 123 us (0.969)
  the two profiles are of different devices: /device:TPU:0 before, /device:TPU:3 now
where the time goes in v5:
time: 123 us; the launch traced here: 124 us
  Pallas kernels  61.2 us (50%)
  starting transfers between devices  31.2 us (25%)
  waiting for transfers between devices  14.6 us (12%)
  other arithmetic  9.76 us (8%)
  local copies, waits for them, and re-layouts  6.06 us (5%)
    pallas_call x1, Pallas kernels, on_device(): pl.pallas_call(functools.partial(sinkhorn_kernel, npairs, d, nbits), grid...  61.2 us
    ppermute x3, waiting for transfers between devices, on_device(): lax.ppermute(halves, 'cols', [(i, i ^ step) for i in range(ncols)])  14.3 us
    all_to_all x1, starting transfers between devices, on_device(): mine = lax.all_to_all(parts, 'cols', 0, 0, tiled=True)  13.3 us
    ppermute x1, starting transfers between devices, on_device(): there = lax.ppermute(here, 'rows', [(0, 1), (1, 0)])  4.75 us
    ppermute x1, starting transfers between devices, on_device(): lax.ppermute(done[kept:], 'rows', swap)  4.74 us
    ppermute x3, starting transfers between devices, on_device(): lax.ppermute(halves, 'cols', [(i, i ^ step) for i in range(ncols)])  4.57 us
    ppermute x1, starting transfers between devices, on_device(): other = lax.ppermute(halves, 'rows', [(0, 1), (1, 0)])  2.76 us
  transfers between devices with their start and end apart: 9, of which 4 were waited for; matrix products, arithmetic and copies ran while one was open for 8% of the time, Pallas kernels for 0%

profile of v5, /device:TPU:3, one launch (start us, length us, event | category | flops | bytes accessed | tf_op | source)
XLA Modules:
  0.0 123.5 jit_solution(15125314785440613684)
XLA Ops:
  0.6 0.0 copy-start
  0.6 0.0 copy-start.2
  0.7 0.0 copy-start.1
  0.7 0.8 copy.25
  1.5 0.8 fusion.19
  2.2 0.7 collective-permute-start
  2.9 0.9 fusion.3
  3.8 2.4 %collective-permute-start.2 = (f32[1,17,1024]{2,1,0:T(8,128)S(1)}, f32[1,17,1024]{2,1,0:T(8,128)S(1)}, u32[]{:S(2)}, u32[]{:S(2)}) collective-permute-start(f32[1,17,1024]{2,1,0:T(8,128)S(1)} %fusion.3), channel_id=1, source_target_pairs={{0,4},{1,5},{2,6},{3,7},{4,0},{5,1},{6,2},{7,3},{8,12},{9,13},{10,... | collective-permute-start | bytes 208904 | tf_op jit(solution)/shard_map/ppermute | solution.py:221
  6.2 1.1 fusion
  7.3 0.4 collective-permute-start.1
  7.7 0.1 fusion.10
  7.8 3.4 %collective-permute-done.2 = f32[1,17,1024]{2,1,0:T(8,128)S(1)} collective-permute-done((f32[1,17,1024]{2,1,0:T(8,128)S(1)}, f32[1,17,1024]{2,1,0:T(8,128)S(1)}, u32[]{:S(2)}, u32[]{:S(2)}) %collective-permute-start.2) | collective-permute-done | bytes 69664 | tf_op jit(solution)/shard_map/ppermute | solution.py:221
  11.2 0.0 copy-done
  11.2 0.0 copy-done.2
  11.2 0.0 copy-done.1
  11.3 0.1 broadcast_select_fusion.5
  11.4 0.9 collective-permute-start.3
  12.3 4.7 %collective-permute-done.3 = f32[2,17,1024]{2,1,0:T(8,128)S(1)} collective-permute-done((f32[2,17,1024]{2,1,0:T(8,128)S(1)}, f32[2,17,1024]{2,1,0:T(8,128)S(1)}, u32[]{:S(2)}, u32[]{:S(2)}) %collective-permute-start.3) | collective-permute-done | bytes 139296 | tf_op jit(solution)/shard_map/ppermute | solution.py:221
  17.0 1.3 %collective-permute-start.4 = (f32[4,17,1024]{2,1,0:T(8,128)S(1)}, f32[4,17,1024]{2,1,0:T(8,128)S(1)}, u32[]{:S(2)}, u32[]{:S(2)}) collective-permute-start(f32[4,17,1024]{2,1,0:T(8,128)S(1)} %pad_maximum_fusion.3), channel_id=1, source_target_pairs={{0,1},{1,0},{2,3},{3,2},{4,5},{5,4},{6,7},{7,6},{8,9},{9,8},{10,11... | collective-permute-start | bytes 835592 | tf_op jit(solution)/shard_map/ppermute | solution.py:221
  18.4 0.6 convert_element_type.25.sel_ref
  19.0 0.1 pad.21.clone
  19.1 0.7 maximum_maximum_fusion.expand_ref
  19.8 6.2 %collective-permute-done.4 = f32[4,17,1024]{2,1,0:T(8,128)S(1)} collective-permute-done((f32[4,17,1024]{2,1,0:T(8,128)S(1)}, f32[4,17,1024]{2,1,0:T(8,128)S(1)}, u32[]{:S(2)}, u32[]{:S(2)}) %collective-permute-start.4) | collective-permute-done | bytes 278560 | tf_op jit(solution)/shard_map/ppermute | solution.py:221
  25.9 0.1 broadcast_select_fusion.1
  26.0 0.1 pad_maximum_fusion.1
  26.1 0.3 copy.27
  26.4 2.8 %collective-permute-start.5 = (f32[8,17,1024]{2,0,1:T(8,128)S(1)}, f32[8,17,1024]{2,0,1:T(8,128)S(1)}, u32[]{:S(2)}, u32[]{:S(2)}) collective-permute-start(f32[8,17,1024]{2,0,1:T(8,128)S(1)} %copy.27), channel_id=1, source_target_pairs={{0,8},{8,0},{1,9},{9,1},{2,10},{10,2},{3,11},{11,3},{4,12},{12,4},... | collective-permute-start | bytes 1671176 | tf_op jit(solution)/shard_map/ppermute | solution.py:225
  29.2 0.0 collective-permute-done
  29.2 0.7 reshape.158.pairs_ref
  29.9 0.8 fusion.16.counts_ref
  30.6 0.0 collective-permute-done.1
  30.7 2.0 %copy.26 = f32[33,4096]{0,1:T(8,128)} copy(f32[33,4096]{1,0:T(8,128)S(1)} %pad_maximum_fusion.2) | data formatting | bytes 1081344 | tf_op jit(solution)/shard_map/concatenate | solution.py:252
  32.7 0.0 collective-permute-done.5
  32.7 0.4 copy_select_fusion.1
  33.1 1.2 %pad_maximum_fusion.blocks_ref = f32[8,34,1024]{2,1,0:T(8,128)} fusion(f32[8,17,1024]{2,1,0:T(8,128)S(1)} %get-tuple-element.13, f32[8,17,1024]{2,1,0:T(8,128)S(1)} %get-tuple-element.12), kind=kLoop, calls=%fused_computation | loop fusion | flops 278528 | bytes 2228224 | tf_op jit(solution)/shard_map/concatenate | solution.py:227
  34.3 61.2 %shard_map.86 = (f32[4096,1]{1,0:T(8,128)}, f32[32,1,256]{2,1,0:T(1,128)}, f32[32,1,256]{2,1,0:T(1,128)}) custom-call(s32[384]{0:T(512)} %reshape.158.pairs_ref, s32[16]{0:T(128)} %fusion.16.counts_ref, f32[4096,33]{1,0:T(8,128)} %bitcast.44, bf16[3,32,128]{2,1,0:T(8,128)(2,1)} %maximum_maximum_fusion.expand_ref, f32[8,128]{1,0:T(8,128)} %convert_element_type.25.sel_ref, ...), custom_call_target="tpu_custom_call" | custom-call | tf_op jit(solution)/shard_map/pallas_call | solution.py:280
  95.5 1.5 %pad_maximum_fusion.6 = f32[8,2,1024]{2,1,0:T(2,128)} fusion(f32[8,1,1024]{2,1,0:T(1,128)} %bitcast.50, f32[8,1,1024]{2,1,0:T(1,128)} %bitcast.49), kind=kLoop, calls=%fused_computation.23 | loop fusion | flops 16384 | bytes 131072 | tf_op jit(solution)/shard_map/stack | solution.py:294
  96.9 13.3 %all-to-all-start = ((f32[8,2,1024]{2,1,0:T(2,128)}), f32[8,2,1024]{2,1,0:T(2,128)S(1)}, u32[]{:S(2)}, u32[]{:S(2)}) async-start(f32[8,2,1024]{2,1,0:T(2,128)} %pad_maximum_fusion.6), calls=%async_computation | async-start | bytes 131072 | tf_op jit(solution)/shard_map/all_to_all | solution.py:295
  110.2 2.1 %slice_reduce_fusion.1 = (f32[2048]{0:T(1024)S(1)}, f32[2048]{0:T(1024)S(1)}) fusion(f32[4096,1]{1,0:T(8,128)} %get-tuple-element.5), kind=kLoop, calls=%fused_computation.2 | loop fusion | bytes 32768 | tf_op jit(solution)/shard_map/slice | solution.py:293
  112.4 4.7 %collective-permute-start.6 = (f32[2048]{0:T(1024)S(1)}, f32[2048]{0:T(1024)S(1)}, u32[]{:S(2)}, u32[]{:S(2)}) collective-permute-start(f32[2048]{0:T(1024)S(1)} %get-tuple-element.9), channel_id=1, source_target_pairs={{0,8},{8,0},{1,9},{9,1},{2,10},{10,2},{3,11},{11,3},{4,12},{12,4},... | collective-permute-start | bytes 24584 | tf_op jit(solution)/shard_map/ppermute | solution.py:293
  117.1 0.0 all-to-all-done
  117.1 0.1 slice_reduce_fusion.2
  117.2 4.7 %collective-permute-start.7 = (f32[2,1024]{1,0:T(2,128)S(1)}, f32[2,1024]{1,0:T(2,128)S(1)}, u32[]{:S(2)}, u32[]{:S(2)}) collective-permute-start(f32[2,1024]{1,0:T(2,128)S(1)} %pad_maximum_fusion.9), channel_id=1, source_target_pairs={{0,8},{8,0},{1,9},{9,1},{2,10},{10,2},{3,11},{11,3},{4,12},{12,4},... | collective-permute-start | bytes 24584 | tf_op jit(solution)/shard_map/ppermute | solution.py:298
  122.0 0.0 collective-permute-done.6
  122.0 0.6 pad_maximum_fusion.7
  122.6 0.2 collective-permute-done.7
  122.9 0.6 add_multiply_fusion
  (19 shorter events, 0.3 us)
Async XLA Ops:
  0.6 10.6 %copy-start = (f32[32,1024]{1,0:T(8,128)S(1)}, f32[32,1024]{1,0:T(8,128)}, u32[]{:S(2)}) copy-start(f32[32,1024]{1,0:T(8,128)} %param.8) | copy-start | bytes 393220
  0.6 10.6 %copy-start.2 = (f32[1024]{0:T(1024)S(1)}, f32[1024]{0:T(1024)}, u32[]{:S(2)}) copy-start(f32[1024]{0:T(1024)} %param.11) | copy-start | bytes 12292
  0.7 10.6 %copy-start.1 = (f32[1024]{0:T(1024)S(1)}, f32[1024]{0:T(1024)}, u32[]{:S(2)}) copy-start(f32[1024]{0:T(1024)} %param.9) | copy-start | bytes 12292
  2.2 27.0 %collective-permute-start = (s32[8,25]{1,0:T(8,128)S(1)}, s32[8,25]{1,0:T(8,128)S(1)}, u32[]{:S(2)}, u32[]{:S(2)}) collective-permute-start(s32[8,25]{1,0:T(8,128)S(1)} %get-tuple-element.28), channel_id=1, source_target_pairs={{0,8},{8,0},{1,9},{9,1},{2,10},{10,2},{3,11},{11,3},{4,12},{12,4},... | collective-permute-start | bytes 2408 | tf_op jit(solution)/shard_map/ppermute | solution.py:254
  3.8 7.4 %collective-permute-start.2 = (f32[1,17,1024]{2,1,0:T(8,128)S(1)}, f32[1,17,1024]{2,1,0:T(8,128)S(1)}, u32[]{:S(2)}, u32[]{:S(2)}) collective-permute-start(f32[1,17,1024]{2,1,0:T(8,128)S(1)} %fusion.3), channel_id=1, source_target_pairs={{0,4},{1,5},{2,6},{3,7},{4,0},{5,1},{6,2},{7,3},{8,12},{9,13},{10,... | collective-permute-start | bytes 208904 | tf_op jit(solution)/shard_map/ppermute | solution.py:221
  7.3 23.3 %collective-permute-start.1 = (f32[33,2048]{1,0:T(8,128)S(1)}, f32[33,2048]{1,0:T(8,128)S(1)}, u32[]{:S(2)}, u32[]{:S(2)}) collective-permute-start(f32[33,2048]{1,0:T(8,128)S(1)} %get-tuple-element.17), channel_id=1, source_target_pairs={{0,8},{8,0},{1,9},{9,1},{2,10},{10,2},{3,11},{11,3},{4,12},{12,4},... | collective-permute-start | bytes 811016 | tf_op jit(solution)/shard_map/ppermute | solution.py:252
  11.4 5.6 %collective-permute-start.3 = (f32[2,17,1024]{2,1,0:T(8,128)S(1)}, f32[2,17,1024]{2,1,0:T(8,128)S(1)}, u32[]{:S(2)}, u32[]{:S(2)}) collective-permute-start(f32[2,17,1024]{2,1,0:T(8,128)S(1)} %pad_maximum_fusion.5), channel_id=1, source_target_pairs={{0,2},{1,3},{2,0},{3,1},{4,6},{5,7},{6,4},{7,5},{8,10},{9,11},{10,... | collective-permute-start | bytes 417800 | tf_op jit(solution)/shard_map/ppermute | solution.py:221
  17.0 8.9 %collective-permute-start.4 = (f32[4,17,1024]{2,1,0:T(8,128)S(1)}, f32[4,17,1024]{2,1,0:T(8,128)S(1)}, u32[]{:S(2)}, u32[]{:S(2)}) collective-permute-start(f32[4,17,1024]{2,1,0:T(8,128)S(1)} %pad_maximum_fusion.3), channel_id=1, source_target_pairs={{0,1},{1,0},{2,3},{3,2},{4,5},{5,4},{6,7},{7,6},{8,9},{9,8},{10,11... | collective-permute-start | bytes 835592 | tf_op jit(solution)/shard_map/ppermute | solution.py:221
  26.4 6.2 %collective-permute-start.5 = (f32[8,17,1024]{2,0,1:T(8,128)S(1)}, f32[8,17,1024]{2,0,1:T(8,128)S(1)}, u32[]{:S(2)}, u32[]{:S(2)}) collective-permute-start(f32[8,17,1024]{2,0,1:T(8,128)S(1)} %copy.27), channel_id=1, source_target_pairs={{0,8},{8,0},{1,9},{9,1},{2,10},{10,2},{3,11},{11,3},{4,12},{12,4},... | collective-permute-start | bytes 1671176 | tf_op jit(solution)/shard_map/ppermute | solution.py:225
  96.9 20.2 %all-to-all-start = ((f32[8,2,1024]{2,1,0:T(2,128)}), f32[8,2,1024]{2,1,0:T(2,128)S(1)}, u32[]{:S(2)}, u32[]{:S(2)}) async-start(f32[8,2,1024]{2,1,0:T(2,128)} %pad_maximum_fusion.6), calls=%async_computation | async-start | bytes 131072 | tf_op jit(solution)/shard_map/all_to_all | solution.py:295
  112.4 9.6 %collective-permute-start.6 = (f32[2048]{0:T(1024)S(1)}, f32[2048]{0:T(1024)S(1)}, u32[]{:S(2)}, u32[]{:S(2)}) collective-permute-start(f32[2048]{0:T(1024)S(1)} %get-tuple-element.9), channel_id=1, source_target_pairs={{0,8},{8,0},{1,9},{9,1},{2,10},{10,2},{3,11},{11,3},{4,12},{12,4},... | collective-permute-start | bytes 24584 | tf_op jit(solution)/shard_map/ppermute | solution.py:293
  117.2 5.6 %collective-permute-start.7 = (f32[2,1024]{1,0:T(2,128)S(1)}, f32[2,1024]{1,0:T(2,128)S(1)}, u32[]{:S(2)}, u32[]{:S(2)}) collective-permute-start(f32[2,1024]{1,0:T(2,128)S(1)} %pad_maximum_fusion.9), channel_id=1, source_target_pairs={{0,8},{8,0},{1,9},{9,1},{2,10},{10,2},{3,11},{11,3},{4,12},{12,4},... | collective-permute-start | bytes 24584 | tf_op jit(solution)/shard_map/ppermute | solution.py:298

commit v6 on v5

--- a/solution.py
+++ b/solution.py
@@ -191,7 +191,23 @@
                    + p2.astype(jnp.float32) * sel[3:4, :]
                    + p3.astype(jnp.float32) * sel[4:5, :]).astype(jnp.bfloat16)
 
-    octets_of(col_pass)
+    def dozens_of(body):
+        def twelve(k, carry):
+            body([12 * k + i for i in range(12)])
+            return carry
+
+        lax.fori_loop(0, cnt // 12, twelve, 0)
+        start = cnt - cnt % 12
+        for size in (8, 4, 2, 1):
+            left = cnt - start
+
+            @pl.when(left >= size)
+            def _part(start=start, size=size):
+                body([start + i for i in range(size)])
+
+            start = start + jnp.where(left >= size, size, 0)
+
+    dozens_of(col_pass)
 
 
 def merge(tops, sums, axis):
@@ -271,7 +287,7 @@
             pl.BlockSpec((tblocks, 1, BLK), lambda b, pr, ct: (0, 0, 0)),
             pl.BlockSpec((tblocks, 1, BLK), lambda b, pr, ct: (0, 0, 0)),
         ],
-        scratch_shapes=[pltpu.VMEM((8, BLK, BLK), jnp.float32),
+        scratch_shapes=[pltpu.VMEM((12, BLK, BLK), jnp.float32),
                         pltpu.VMEM((BLK, KP), jnp.bfloat16),
                         pltpu.VMEM((BLK, KP), jnp.bfloat16),
                         pltpu.VMEM((8, BLK, LANE), jnp.float32),

time: 123 us -> 118 us (0.959)
  the two profiles are of different devices: /device:TPU:3 before, /device:TPU:0 now
where the time goes in v6:
time: 118 us
  Pallas kernels  60.2 us (51%)
  waiting for transfers between devices  22.4 us (19%)
  starting transfers between devices  18.6 us (16%)
  other arithmetic  9.83 us (8%)
  local copies, waits for them, and re-layouts  6.05 us (5%)
    pallas_call x1, Pallas kernels, on_device(): pl.pallas_call(functools.partial(sinkhorn_kernel, npairs, d, nbits), grid...  60.2 us
    ppermute x3, waiting for transfers between devices, on_device(): lax.ppermute(halves, 'cols', [(i, i ^ step) for i in range(ncols)])  17.2 us
    all_to_all x1, starting transfers between devices, on_device(): mine = lax.all_to_all(parts, 'cols', 0, 0, tiled=True)  11.8 us
    ppermute x3, starting transfers between devices, on_device(): lax.ppermute(halves, 'cols', [(i, i ^ step) for i in range(ncols)])  5.93 us
    all_to_all x1, waiting for transfers between devices, on_device(): mine = lax.all_to_all(parts, 'cols', 0, 0, tiled=True)  4.67 us
  transfers between devices with their start and end apart: 9, of which 5 were waited for; matrix products, arithmetic and copies ran while one was open for 9% of the time, Pallas kernels for 0%

profile of v6, /device:TPU:0, one launch (start us, length us, event | category | flops | bytes accessed | tf_op | source)
XLA Modules:
  0.0 117.9 jit_solution(6498576953241244175)
XLA Ops:
  0.6 0.0 copy-start
  0.6 0.0 copy-start.2
  0.7 0.0 copy-start.1
  0.7 0.8 copy.25
  1.5 0.8 fusion.19
  2.2 0.5 collective-permute-start
  2.7 1.0 fusion.3
  3.7 3.7 %collective-permute-start.2 = (f32[1,17,1024]{2,1,0:T(8,128)S(1)}, f32[1,17,1024]{2,1,0:T(8,128)S(1)}, u32[]{:S(2)}, u32[]{:S(2)}) collective-permute-start(f32[1,17,1024]{2,1,0:T(8,128)S(1)} %fusion.3), channel_id=1, source_target_pairs={{0,4},{1,5},{2,6},{3,7},{4,0},{5,1},{6,2},{7,3},{8,12},{9,13},{10,... | collective-permute-start | bytes 208904 | tf_op jit(solution)/shard_map/ppermute | solution.py:237
  7.3 1.1 fusion
  8.4 0.2 collective-permute-start.1
  8.7 0.1 fusion.10
  8.7 4.1 %collective-permute-done.2 = f32[1,17,1024]{2,1,0:T(8,128)S(1)} collective-permute-done((f32[1,17,1024]{2,1,0:T(8,128)S(1)}, f32[1,17,1024]{2,1,0:T(8,128)S(1)}, u32[]{:S(2)}, u32[]{:S(2)}) %collective-permute-start.2) | collective-permute-done | bytes 69664 | tf_op jit(solution)/shard_map/ppermute | solution.py:237
  12.8 0.0 copy-done
  12.8 0.0 copy-done.2
  12.8 0.0 copy-done.1
  12.8 0.1 broadcast_select_fusion.5
  12.9 0.8 collective-permute-start.3
  13.8 5.9 %collective-permute-done.3 = f32[2,17,1024]{2,1,0:T(8,128)S(1)} collective-permute-done((f32[2,17,1024]{2,1,0:T(8,128)S(1)}, f32[2,17,1024]{2,1,0:T(8,128)S(1)}, u32[]{:S(2)}, u32[]{:S(2)}) %collective-permute-start.3) | collective-permute-done | bytes 139296 | tf_op jit(solution)/shard_map/ppermute | solution.py:237
  19.7 1.4 %collective-permute-start.4 = (f32[4,17,1024]{2,1,0:T(8,128)S(1)}, f32[4,17,1024]{2,1,0:T(8,128)S(1)}, u32[]{:S(2)}, u32[]{:S(2)}) collective-permute-start(f32[4,17,1024]{2,1,0:T(8,128)S(1)} %pad_maximum_fusion.3), channel_id=1, source_target_pairs={{0,1},{1,0},{2,3},{3,2},{4,5},{5,4},{6,7},{7,6},{8,9},{9,8},{10,11... | collective-permute-start | bytes 835592 | tf_op jit(solution)/shard_map/ppermute | solution.py:237
  21.2 0.6 convert_element_type.25.sel_ref
  21.8 0.1 pad.21.clone
  21.9 0.7 maximum_maximum_fusion.expand_ref
  22.6 7.2 %collective-permute-done.4 = f32[4,17,1024]{2,1,0:T(8,128)S(1)} collective-permute-done((f32[4,17,1024]{2,1,0:T(8,128)S(1)}, f32[4,17,1024]{2,1,0:T(8,128)S(1)}, u32[]{:S(2)}, u32[]{:S(2)}) %collective-permute-start.4) | collective-permute-done | bytes 278560 | tf_op jit(solution)/shard_map/ppermute | solution.py:237
  29.8 0.1 broadcast_select_fusion.1
  29.9 0.1 pad_maximum_fusion.1
  29.9 0.3 copy.27
  30.3 0.1 collective-permute-start.5
  30.4 0.0 collective-permute-done
  30.4 0.7 reshape.158.pairs_ref
  31.0 0.8 fusion.16.counts_ref
  31.8 0.0 collective-permute-done.1
  31.9 2.0 %copy.26 = f32[33,4096]{0,1:T(8,128)} copy(f32[33,4096]{1,0:T(8,128)S(1)} %pad_maximum_fusion.2) | data formatting | bytes 1081344 | tf_op jit(solution)/shard_map/concatenate | solution.py:268
  33.8 0.0 collective-permute-done.5
  33.8 0.4 copy_select_fusion.1
  34.2 1.2 %pad_maximum_fusion.blocks_ref = f32[8,34,1024]{2,1,0:T(8,128)} fusion(f32[8,17,1024]{2,1,0:T(8,128)S(1)} %get-tuple-element.13, f32[8,17,1024]{2,1,0:T(8,128)S(1)} %get-tuple-element.12), kind=kLoop, calls=%fused_computation | loop fusion | flops 278528 | bytes 2228224 | tf_op jit(solution)/shard_map/concatenate | solution.py:243
  35.5 60.2 %shard_map.86 = (f32[4096,1]{1,0:T(8,128)}, f32[32,1,256]{2,1,0:T(1,128)}, f32[32,1,256]{2,1,0:T(1,128)}) custom-call(s32[384]{0:T(512)} %reshape.158.pairs_ref, s32[16]{0:T(128)} %fusion.16.counts_ref, f32[4096,33]{1,0:T(8,128)} %bitcast.44, bf16[3,32,128]{2,1,0:T(8,128)(2,1)} %maximum_maximum_fusion.expand_ref, f32[8,128]{1,0:T(8,128)} %convert_element_type.25.sel_ref, ...), custom_call_target="tpu_custom_call" | custom-call | tf_op jit(solution)/shard_map/pallas_call | solution.py:296
  95.7 1.5 %pad_maximum_fusion.6 = f32[8,2,1024]{2,1,0:T(2,128)} fusion(f32[8,1,1024]{2,1,0:T(1,128)} %bitcast.50, f32[8,1,1024]{2,1,0:T(1,128)} %bitcast.49), kind=kLoop, calls=%fused_computation.23 | loop fusion | flops 16384 | bytes 131072 | tf_op jit(solution)/shard_map/stack | solution.py:310
  97.2 11.8 %all-to-all-start = ((f32[8,2,1024]{2,1,0:T(2,128)}), f32[8,2,1024]{2,1,0:T(2,128)S(1)}, u32[]{:S(2)}, u32[]{:S(2)}) async-start(f32[8,2,1024]{2,1,0:T(2,128)} %pad_maximum_fusion.6), calls=%async_computation | async-start | bytes 131072 | tf_op jit(solution)/shard_map/all_to_all | solution.py:311
  108.9 2.1 %slice_reduce_fusion.1 = (f32[2048]{0:T(1024)S(1)}, f32[2048]{0:T(1024)S(1)}) fusion(f32[4096,1]{1,0:T(8,128)} %get-tuple-element.5), kind=kLoop, calls=%fused_computation.2 | loop fusion | bytes 32768 | tf_op jit(solution)/shard_map/slice | solution.py:309
  111.1 0.1 collective-permute-start.6
  111.2 4.7 %all-to-all-done = f32[8,2,1024]{2,1,0:T(2,128)S(1)} async-done(((f32[8,2,1024]{2,1,0:T(2,128)}), f32[8,2,1024]{2,1,0:T(2,128)S(1)}, u32[]{:S(2)}, u32[]{:S(2)}) %all-to-all-start) | async-done | bytes 65568 | tf_op jit(solution)/shard_map/all_to_all | solution.py:311
  115.9 0.1 slice_reduce_fusion.2
  116.0 0.1 collective-permute-start.7
  116.1 0.0 collective-permute-done.6
  116.1 0.6 pad_maximum_fusion.7
  116.7 0.5 collective-permute-done.7
  117.3 0.6 add_multiply_fusion
  (19 shorter events, 0.3 us)
Async XLA Ops:
  0.6 12.2 %copy-start = (f32[32,1024]{1,0:T(8,128)S(1)}, f32[32,1024]{1,0:T(8,128)}, u32[]{:S(2)}) copy-start(f32[32,1024]{1,0:T(8,128)} %param.8) | copy-start | bytes 393220
  0.6 12.2 %copy-start.2 = (f32[1024]{0:T(1024)S(1)}, f32[1024]{0:T(1024)}, u32[]{:S(2)}) copy-start(f32[1024]{0:T(1024)} %param.11) | copy-start | bytes 12292
  0.7 12.2 %copy-start.1 = (f32[1024]{0:T(1024)S(1)}, f32[1024]{0:T(1024)}, u32[]{:S(2)}) copy-start(f32[1024]{0:T(1024)} %param.9) | copy-start | bytes 12292
  2.2 28.1 %collective-permute-start = (s32[8,25]{1,0:T(8,128)S(1)}, s32[8,25]{1,0:T(8,128)S(1)}, u32[]{:S(2)}, u32[]{:S(2)}) collective-permute-start(s32[8,25]{1,0:T(8,128)S(1)} %get-tuple-element.28), channel_id=1, source_target_pairs={{0,8},{8,0},{1,9},{9,1},{2,10},{10,2},{3,11},{11,3},{4,12},{12,4},... | collective-permute-start | bytes 2408 | tf_op jit(solution)/shard_map/ppermute | solution.py:270
  3.7 9.2 %collective-permute-start.2 = (f32[1,17,1024]{2,1,0:T(8,128)S(1)}, f32[1,17,1024]{2,1,0:T(8,128)S(1)}, u32[]{:S(2)}, u32[]{:S(2)}) collective-permute-start(f32[1,17,1024]{2,1,0:T(8,128)S(1)} %fusion.3), channel_id=1, source_target_pairs={{0,4},{1,5},{2,6},{3,7},{4,0},{5,1},{6,2},{7,3},{8,12},{9,13},{10,... | collective-permute-start | bytes 208904 | tf_op jit(solution)/shard_map/ppermute | solution.py:237
  8.4 23.4 %collective-permute-start.1 = (f32[33,2048]{1,0:T(8,128)S(1)}, f32[33,2048]{1,0:T(8,128)S(1)}, u32[]{:S(2)}, u32[]{:S(2)}) collective-permute-start(f32[33,2048]{1,0:T(8,128)S(1)} %get-tuple-element.17), channel_id=1, source_target_pairs={{0,8},{8,0},{1,9},{9,1},{2,10},{10,2},{3,11},{11,3},{4,12},{12,4},... | collective-permute-start | bytes 811016 | tf_op jit(solution)/shard_map/ppermute | solution.py:268
  12.9 6.7 %collective-permute-start.3 = (f32[2,17,1024]{2,1,0:T(8,128)S(1)}, f32[2,17,1024]{2,1,0:T(8,128)S(1)}, u32[]{:S(2)}, u32[]{:S(2)}) collective-permute-start(f32[2,17,1024]{2,1,0:T(8,128)S(1)} %pad_maximum_fusion.5), channel_id=1, source_target_pairs={{0,2},{1,3},{2,0},{3,1},{4,6},{5,7},{6,4},{7,5},{8,10},{9,11},{10,... | collective-permute-start | bytes 417800 | tf_op jit(solution)/shard_map/ppermute | solution.py:237
  19.7 10.1 %collective-permute-start.4 = (f32[4,17,1024]{2,1,0:T(8,128)S(1)}, f32[4,17,1024]{2,1,0:T(8,128)S(1)}, u32[]{:S(2)}, u32[]{:S(2)}) collective-permute-start(f32[4,17,1024]{2,1,0:T(8,128)S(1)} %pad_maximum_fusion.3), channel_id=1, source_target_pairs={{0,1},{1,0},{2,3},{3,2},{4,5},{5,4},{6,7},{7,6},{8,9},{9,8},{10,11... | collective-permute-start | bytes 835592 | tf_op jit(solution)/shard_map/ppermute | solution.py:237
  30.3 3.6 %collective-permute-start.5 = (f32[8,17,1024]{2,0,1:T(8,128)S(1)}, f32[8,17,1024]{2,0,1:T(8,128)S(1)}, u32[]{:S(2)}, u32[]{:S(2)}) collective-permute-start(f32[8,17,1024]{2,0,1:T(8,128)S(1)} %copy.27), channel_id=1, source_target_pairs={{0,8},{8,0},{1,9},{9,1},{2,10},{10,2},{3,11},{11,3},{4,12},{12,4},... | collective-permute-start | bytes 1671176 | tf_op jit(solution)/shard_map/ppermute | solution.py:241
  97.2 18.7 %all-to-all-start = ((f32[8,2,1024]{2,1,0:T(2,128)}), f32[8,2,1024]{2,1,0:T(2,128)S(1)}, u32[]{:S(2)}, u32[]{:S(2)}) async-start(f32[8,2,1024]{2,1,0:T(2,128)} %pad_maximum_fusion.6), calls=%async_computation | async-start | bytes 131072 | tf_op jit(solution)/shard_map/all_to_all | solution.py:311
  111.1 5.0 %collective-permute-start.6 = (f32[2048]{0:T(1024)S(1)}, f32[2048]{0:T(1024)S(1)}, u32[]{:S(2)}, u32[]{:S(2)}) collective-permute-start(f32[2048]{0:T(1024)S(1)} %get-tuple-element.9), channel_id=1, source_target_pairs={{0,8},{8,0},{1,9},{9,1},{2,10},{10,2},{3,11},{11,3},{4,12},{12,4},... | collective-permute-start | bytes 24584 | tf_op jit(solution)/shard_map/ppermute | solution.py:309
  116.0 1.2 %collective-permute-start.7 = (f32[2,1024]{1,0:T(2,128)S(1)}, f32[2,1024]{1,0:T(2,128)S(1)}, u32[]{:S(2)}, u32[]{:S(2)}) collective-permute-start(f32[2,1024]{1,0:T(2,128)S(1)} %pad_maximum_fusion.9), channel_id=1, source_target_pairs={{0,8},{8,0},{1,9},{9,1},{2,10},{10,2},{3,11},{11,3},{4,12},{12,4},... | collective-permute-start | bytes 24584 | tf_op jit(solution)/shard_map/ppermute | solution.py:314

commit v7 on v5

--- a/solution.py
+++ b/solution.py
@@ -90,7 +90,7 @@
           + jnp.dot(x3, expand_ref[2], preferred_element_type=jnp.float32))
     sel = sel_ref[...]
     xr_ref[...] = (xa + sel[0:1, :]).astype(jnp.bfloat16)
-    for a in range(4):
+    for a in range(6):
         acc_ref[2 * a] = jnp.full((BLK, LANE), NEG, jnp.float32)
         acc_ref[2 * a + 1] = jnp.zeros((BLK, LANE), jnp.float32)
 
@@ -175,14 +175,30 @@
         def _last():
             body([cnt - 1])
 
-    octets_of(row_pass)
-    tops = [acc_ref[2 * a] for a in range(4)]
+    def dozens_of(body):
+        def twelve(k, carry):
+            body([12 * k + i for i in range(12)])
+            return carry
+
+        lax.fori_loop(0, cnt // 12, twelve, 0)
+        start = cnt - cnt % 12
+        for size in (8, 4, 2, 1):
+            left = cnt - start
+
+            @pl.when(left >= size)
+            def _part(start=start, size=size):
+                body([start + i for i in range(size)])
+
+            start = start + jnp.where(left >= size, size, 0)
+
+    dozens_of(row_pass)
+    tops = [acc_ref[2 * a] for a in range(6)]
     lane_top = tops[0]
     for t in tops[1:]:
         lane_top = jnp.maximum(lane_top, t)
     m = jnp.max(lane_top, axis=1, keepdims=True)
     lane_sum = acc_ref[1] * jnp.exp2(tops[0] - m)
-    for a in range(1, 4):
+    for a in range(1, 6):
         lane_sum = lane_sum + acc_ref[2 * a + 1] * jnp.exp2(tops[a] - m)
     lse = m + jnp.log2(jnp.sum(lane_sum, axis=1, keepdims=True))
     fpot_ref[...] = xn - (epsilon * LN2) * lse
@@ -191,7 +207,7 @@
                    + p2.astype(jnp.float32) * sel[3:4, :]
                    + p3.astype(jnp.float32) * sel[4:5, :]).astype(jnp.bfloat16)
 
-    octets_of(col_pass)
+    dozens_of(col_pass)
 
 
 def merge(tops, sums, axis):
@@ -271,10 +287,10 @@
             pl.BlockSpec((tblocks, 1, BLK), lambda b, pr, ct: (0, 0, 0)),
             pl.BlockSpec((tblocks, 1, BLK), lambda b, pr, ct: (0, 0, 0)),
         ],
-        scratch_shapes=[pltpu.VMEM((8, BLK, BLK), jnp.float32),
+        scratch_shapes=[pltpu.VMEM((12, BLK, BLK), jnp.float32),
                         pltpu.VMEM((BLK, KP), jnp.bfloat16),
                         pltpu.VMEM((BLK, KP), jnp.bfloat16),
-                        pltpu.VMEM((8, BLK, LANE), jnp.float32),
+                        pltpu.VMEM((12, BLK, LANE), jnp.float32),
                         pltpu.VMEM((tblocks, KP, BLK), jnp.bfloat16)],
     )
     fpot, gtop, gsum = pl.pallas_call(

time: 123 us -> 118 us (0.959)
  the two profiles are of different devices: /device:TPU:3 before, /device:TPU:0 now
where the time goes in v7:
time: 118 us; the launch traced here: 117 us
  Pallas kernels  54.3 us (46%)
  starting transfers between devices  24.2 us (21%)
  waiting for transfers between devices  21.5 us (18%)
  other arithmetic  9.83 us (8%)
  local copies, waits for them, and re-layouts  6.05 us (5%)
    pallas_call x1, Pallas kernels, on_device(): pl.pallas_call(functools.partial(sinkhorn_kernel, npairs, d, nbits), grid...  54.3 us
    ppermute x3, waiting for transfers between devices, on_device(): lax.ppermute(halves, 'cols', [(i, i ^ step) for i in range(ncols)])  17.2 us
    all_to_all x1, starting transfers between devices, on_device(): mine = lax.all_to_all(parts, 'cols', 0, 0, tiled=True)  16.1 us
    ppermute x3, starting transfers between devices, on_device(): lax.ppermute(halves, 'cols', [(i, i ^ step) for i in range(ncols)])  5.93 us
    all_to_all x1, waiting for transfers between devices, on_device(): mine = lax.all_to_all(parts, 'cols', 0, 0, tiled=True)  3.88 us
  transfers between devices with their start and end apart: 9, of which 5 were waited for; matrix products, arithmetic and copies ran while one was open for 9% of the time, Pallas kernels for 0%

profile of v7, /device:TPU:0, one launch (start us, length us, event | category | flops | bytes accessed | tf_op | source)
XLA Modules:
  0.0 116.7 jit_solution(7101011473420249306)
XLA Ops:
  0.6 0.0 copy-start
  0.6 0.0 copy-start.2
  0.7 0.0 copy-start.1
  0.7 0.8 copy.25
  1.5 0.8 fusion.19
  2.2 0.5 collective-permute-start
  2.7 1.0 fusion.3
  3.7 3.7 %collective-permute-start.2 = (f32[1,17,1024]{2,1,0:T(8,128)S(1)}, f32[1,17,1024]{2,1,0:T(8,128)S(1)}, u32[]{:S(2)}, u32[]{:S(2)}) collective-permute-start(f32[1,17,1024]{2,1,0:T(8,128)S(1)} %fusion.3), channel_id=1, source_target_pairs={{0,4},{1,5},{2,6},{3,7},{4,0},{5,1},{6,2},{7,3},{8,12},{9,13},{10,... | collective-permute-start | bytes 208904 | tf_op jit(solution)/shard_map/ppermute | solution.py:237
  7.3 1.1 fusion
  8.4 0.2 collective-permute-start.1
  8.7 0.1 fusion.10
  8.7 4.1 %collective-permute-done.2 = f32[1,17,1024]{2,1,0:T(8,128)S(1)} collective-permute-done((f32[1,17,1024]{2,1,0:T(8,128)S(1)}, f32[1,17,1024]{2,1,0:T(8,128)S(1)}, u32[]{:S(2)}, u32[]{:S(2)}) %collective-permute-start.2) | collective-permute-done | bytes 69664 | tf_op jit(solution)/shard_map/ppermute | solution.py:237
  12.8 0.0 copy-done
  12.8 0.0 copy-done.2
  12.8 0.0 copy-done.1
  12.8 0.1 broadcast_select_fusion.5
  12.9 0.8 collective-permute-start.3
  13.8 5.9 %collective-permute-done.3 = f32[2,17,1024]{2,1,0:T(8,128)S(1)} collective-permute-done((f32[2,17,1024]{2,1,0:T(8,128)S(1)}, f32[2,17,1024]{2,1,0:T(8,128)S(1)}, u32[]{:S(2)}, u32[]{:S(2)}) %collective-permute-start.3) | collective-permute-done | bytes 139296 | tf_op jit(solution)/shard_map/ppermute | solution.py:237
  19.7 1.4 %collective-permute-start.4 = (f32[4,17,1024]{2,1,0:T(8,128)S(1)}, f32[4,17,1024]{2,1,0:T(8,128)S(1)}, u32[]{:S(2)}, u32[]{:S(2)}) collective-permute-start(f32[4,17,1024]{2,1,0:T(8,128)S(1)} %pad_maximum_fusion.3), channel_id=1, source_target_pairs={{0,1},{1,0},{2,3},{3,2},{4,5},{5,4},{6,7},{7,6},{8,9},{9,8},{10,11... | collective-permute-start | bytes 835592 | tf_op jit(solution)/shard_map/ppermute | solution.py:237
  21.2 0.6 convert_element_type.25.sel_ref
  21.8 0.1 pad.21.clone
  21.9 0.7 maximum_maximum_fusion.expand_ref
  22.6 7.2 %collective-permute-done.4 = f32[4,17,1024]{2,1,0:T(8,128)S(1)} collective-permute-done((f32[4,17,1024]{2,1,0:T(8,128)S(1)}, f32[4,17,1024]{2,1,0:T(8,128)S(1)}, u32[]{:S(2)}, u32[]{:S(2)}) %collective-permute-start.4) | collective-permute-done | bytes 278560 | tf_op jit(solution)/shard_map/ppermute | solution.py:237
  29.8 0.1 broadcast_select_fusion.1
  29.9 0.1 pad_maximum_fusion.1
  29.9 0.3 copy.27
  30.3 0.1 collective-permute-start.5
  30.4 0.0 collective-permute-done
  30.4 0.7 reshape.158.pairs_ref
  31.0 0.8 fusion.16.counts_ref
  31.8 0.0 collective-permute-done.1
  31.9 2.0 %copy.26 = f32[33,4096]{0,1:T(8,128)} copy(f32[33,4096]{1,0:T(8,128)S(1)} %pad_maximum_fusion.2) | data formatting | bytes 1081344 | tf_op jit(solution)/shard_map/concatenate | solution.py:268
  33.8 0.0 collective-permute-done.5
  33.8 0.4 copy_select_fusion.1
  34.2 1.2 %pad_maximum_fusion.blocks_ref = f32[8,34,1024]{2,1,0:T(8,128)} fusion(f32[8,17,1024]{2,1,0:T(8,128)S(1)} %get-tuple-element.13, f32[8,17,1024]{2,1,0:T(8,128)S(1)} %get-tuple-element.12), kind=kLoop, calls=%fused_computation | loop fusion | flops 278528 | bytes 2228224 | tf_op jit(solution)/shard_map/concatenate | solution.py:243
  35.5 54.3 %shard_map.86 = (f32[4096,1]{1,0:T(8,128)}, f32[32,1,256]{2,1,0:T(1,128)}, f32[32,1,256]{2,1,0:T(1,128)}) custom-call(s32[384]{0:T(512)} %reshape.158.pairs_ref, s32[16]{0:T(128)} %fusion.16.counts_ref, f32[4096,33]{1,0:T(8,128)} %bitcast.44, bf16[3,32,128]{2,1,0:T(8,128)(2,1)} %maximum_maximum_fusion.expand_ref, f32[8,128]{1,0:T(8,128)} %convert_element_type.25.sel_ref, ...), custom_call_target="tpu_custom_call" | custom-call | tf_op jit(solution)/shard_map/pallas_call | solution.py:296
  89.8 1.5 %pad_maximum_fusion.6 = f32[8,2,1024]{2,1,0:T(2,128)} fusion(f32[8,1,1024]{2,1,0:T(1,128)} %bitcast.50, f32[8,1,1024]{2,1,0:T(1,128)} %bitcast.49), kind=kLoop, calls=%fused_computation.23 | loop fusion | flops 16384 | bytes 131072 | tf_op jit(solution)/shard_map/stack | solution.py:310
  91.3 16.1 %all-to-all-start = ((f32[8,2,1024]{2,1,0:T(2,128)}), f32[8,2,1024]{2,1,0:T(2,128)S(1)}, u32[]{:S(2)}, u32[]{:S(2)}) async-start(f32[8,2,1024]{2,1,0:T(2,128)} %pad_maximum_fusion.6), calls=%async_computation | async-start | bytes 131072 | tf_op jit(solution)/shard_map/all_to_all | solution.py:311
  107.4 2.1 %slice_reduce_fusion.1 = (f32[2048]{0:T(1024)S(1)}, f32[2048]{0:T(1024)S(1)}) fusion(f32[4096,1]{1,0:T(8,128)} %get-tuple-element.5), kind=kLoop, calls=%fused_computation.2 | loop fusion | bytes 32768 | tf_op jit(solution)/shard_map/slice | solution.py:309
  109.6 1.2 %collective-permute-start.6 = (f32[2048]{0:T(1024)S(1)}, f32[2048]{0:T(1024)S(1)}, u32[]{:S(2)}, u32[]{:S(2)}) collective-permute-start(f32[2048]{0:T(1024)S(1)} %get-tuple-element.9), channel_id=1, source_target_pairs={{0,8},{8,0},{1,9},{9,1},{2,10},{10,2},{3,11},{11,3},{4,12},{12,4},... | collective-permute-start | bytes 24584 | tf_op jit(solution)/shard_map/ppermute | solution.py:309
  110.7 3.9 %all-to-all-done = f32[8,2,1024]{2,1,0:T(2,128)S(1)} async-done(((f32[8,2,1024]{2,1,0:T(2,128)}), f32[8,2,1024]{2,1,0:T(2,128)S(1)}, u32[]{:S(2)}, u32[]{:S(2)}) %all-to-all-start) | async-done | bytes 65568 | tf_op jit(solution)/shard_map/all_to_all | solution.py:311
  114.6 0.1 slice_reduce_fusion.2
  114.7 0.2 collective-permute-start.7
  114.9 0.0 collective-permute-done.6
  114.9 0.6 pad_maximum_fusion.7
  115.5 0.4 collective-permute-done.7
  116.1 0.6 add_multiply_fusion
  (19 shorter events, 0.3 us)
Async XLA Ops:
  0.6 12.2 %copy-start = (f32[32,1024]{1,0:T(8,128)S(1)}, f32[32,1024]{1,0:T(8,128)}, u32[]{:S(2)}) copy-start(f32[32,1024]{1,0:T(8,128)} %param.8) | copy-start | bytes 393220
  0.6 12.2 %copy-start.2 = (f32[1024]{0:T(1024)S(1)}, f32[1024]{0:T(1024)}, u32[]{:S(2)}) copy-start(f32[1024]{0:T(1024)} %param.11) | copy-start | bytes 12292
  0.7 12.2 %copy-start.1 = (f32[1024]{0:T(1024)S(1)}, f32[1024]{0:T(1024)}, u32[]{:S(2)}) copy-start(f32[1024]{0:T(1024)} %param.9) | copy-start | bytes 12292
  2.2 28.1 %collective-permute-start = (s32[8,25]{1,0:T(8,128)S(1)}, s32[8,25]{1,0:T(8,128)S(1)}, u32[]{:S(2)}, u32[]{:S(2)}) collective-permute-start(s32[8,25]{1,0:T(8,128)S(1)} %get-tuple-element.28), channel_id=1, source_target_pairs={{0,8},{8,0},{1,9},{9,1},{2,10},{10,2},{3,11},{11,3},{4,12},{12,4},... | collective-permute-start | bytes 2408 | tf_op jit(solution)/shard_map/ppermute | solution.py:270
  3.7 9.2 %collective-permute-start.2 = (f32[1,17,1024]{2,1,0:T(8,128)S(1)}, f32[1,17,1024]{2,1,0:T(8,128)S(1)}, u32[]{:S(2)}, u32[]{:S(2)}) collective-permute-start(f32[1,17,1024]{2,1,0:T(8,128)S(1)} %fusion.3), channel_id=1, source_target_pairs={{0,4},{1,5},{2,6},{3,7},{4,0},{5,1},{6,2},{7,3},{8,12},{9,13},{10,... | collective-permute-start | bytes 208904 | tf_op jit(solution)/shard_map/ppermute | solution.py:237
  8.4 23.4 %collective-permute-start.1 = (f32[33,2048]{1,0:T(8,128)S(1)}, f32[33,2048]{1,0:T(8,128)S(1)}, u32[]{:S(2)}, u32[]{:S(2)}) collective-permute-start(f32[33,2048]{1,0:T(8,128)S(1)} %get-tuple-element.17), channel_id=1, source_target_pairs={{0,8},{8,0},{1,9},{9,1},{2,10},{10,2},{3,11},{11,3},{4,12},{12,4},... | collective-permute-start | bytes 811016 | tf_op jit(solution)/shard_map/ppermute | solution.py:268
  12.9 6.7 %collective-permute-start.3 = (f32[2,17,1024]{2,1,0:T(8,128)S(1)}, f32[2,17,1024]{2,1,0:T(8,128)S(1)}, u32[]{:S(2)}, u32[]{:S(2)}) collective-permute-start(f32[2,17,1024]{2,1,0:T(8,128)S(1)} %pad_maximum_fusion.5), channel_id=1, source_target_pairs={{0,2},{1,3},{2,0},{3,1},{4,6},{5,7},{6,4},{7,5},{8,10},{9,11},{10,... | collective-permute-start | bytes 417800 | tf_op jit(solution)/shard_map/ppermute | solution.py:237
  19.7 10.1 %collective-permute-start.4 = (f32[4,17,1024]{2,1,0:T(8,128)S(1)}, f32[4,17,1024]{2,1,0:T(8,128)S(1)}, u32[]{:S(2)}, u32[]{:S(2)}) collective-permute-start(f32[4,17,1024]{2,1,0:T(8,128)S(1)} %pad_maximum_fusion.3), channel_id=1, source_target_pairs={{0,1},{1,0},{2,3},{3,2},{4,5},{5,4},{6,7},{7,6},{8,9},{9,8},{10,11... | collective-permute-start | bytes 835592 | tf_op jit(solution)/shard_map/ppermute | solution.py:237
  30.3 3.6 %collective-permute-start.5 = (f32[8,17,1024]{2,0,1:T(8,128)S(1)}, f32[8,17,1024]{2,0,1:T(8,128)S(1)}, u32[]{:S(2)}, u32[]{:S(2)}) collective-permute-start(f32[8,17,1024]{2,0,1:T(8,128)S(1)} %copy.27), channel_id=1, source_target_pairs={{0,8},{8,0},{1,9},{9,1},{2,10},{10,2},{3,11},{11,3},{4,12},{12,4},... | collective-permute-start | bytes 1671176 | tf_op jit(solution)/shard_map/ppermute | solution.py:241
  91.3 23.3 %all-to-all-start = ((f32[8,2,1024]{2,1,0:T(2,128)}), f32[8,2,1024]{2,1,0:T(2,128)S(1)}, u32[]{:S(2)}, u32[]{:S(2)}) async-start(f32[8,2,1024]{2,1,0:T(2,128)} %pad_maximum_fusion.6), calls=%async_computation | async-start | bytes 131072 | tf_op jit(solution)/shard_map/all_to_all | solution.py:311
  109.6 5.4 %collective-permute-start.6 = (f32[2048]{0:T(1024)S(1)}, f32[2048]{0:T(1024)S(1)}, u32[]{:S(2)}, u32[]{:S(2)}) collective-permute-start(f32[2048]{0:T(1024)S(1)} %get-tuple-element.9), channel_id=1, source_target_pairs={{0,8},{8,0},{1,9},{9,1},{2,10},{10,2},{3,11},{11,3},{4,12},{12,4},... | collective-permute-start | bytes 24584 | tf_op jit(solution)/shard_map/ppermute | solution.py:309
  114.7 1.2 %collective-permute-start.7 = (f32[2,1024]{1,0:T(2,128)S(1)}, f32[2,1024]{1,0:T(2,128)S(1)}, u32[]{:S(2)}, u32[]{:S(2)}) collective-permute-start(f32[2,1024]{1,0:T(2,128)S(1)} %pad_maximum_fusion.9), channel_id=1, source_target_pairs={{0,8},{8,0},{1,9},{9,1},{2,10},{10,2},{3,11},{11,3},{4,12},{12,4},... | collective-permute-start | bytes 24584 | tf_op jit(solution)/shard_map/ppermute | solution.py:314
